TPU v7x, 256 devices: a whole 4x4x8 slice. The times are simulated.
256 devices in a mesh: row: 4 (over y), col: 64 (over x, z, core).
Axes of the slice: x: 4, y: 4, z: 8, core: 2. Of those that a mesh axis runs over, the one named last changes fastest.
Arguments:
- features: bfloat16 [2097152, 128], P(('row', 'col')), may hold values from -6 to 6
- position: float32 [3, 2097152], P(None, ('row', 'col')), may hold values from -6 to 6
- velocity: float32 [3, 2097152], P(None, ('row', 'col')), may hold values from -6 to 6
- noise: float32 [3, 2097152], P(None, ('row', 'col')), may hold values from -6 to 6
- charge: float32 [2097152], P(('row', 'col')), may hold values from -18 to 18
- frac: float32 [3, 2097152], P(None, ('row', 'col')), may hold values from 0 to 1
- cell: int32 [3, 2097152], P(None, ('row', 'col')), may hold values from 0 to 511, as said below
- dest: int32 [2097152, 1], P(('row', 'col')), may hold values from 0 to 63; in each aligned block of 8192 rows (0 to 8191, 8192 to 16383, ...) at most 256 rows name the same one
- w_in: bfloat16 [128, 256], replicated, may hold values from -0.5 to 0.5
- w_out: bfloat16 [256, 128], replicated, may hold values from -0.375 to 0.375
- w_force: bfloat16 [3, 256], replicated, may hold values from -0.375 to 0.375
Outputs:
- arrived_feat: bfloat16 [4194304, 128], P(('row', 'col'))
- arrived_state: float32 [6, 4194304], P(None, ('row', 'col'))
- spectrum: float32 [2, 128, 512, 512], P(None, 'row', 'col')
Inputs may be any that keep to these rules, and one draw needn't show every extreme that they name: For the atom held by device d, cell[0] lies in [(d // 64) * 32, (d // 64 + 1) * 32) and cell[2] in [(d % 64) * 8, (d % 64 + 1) * 8); cell[1] is any cell along y. `dest`: among the atoms of one device no value is named by more than 256 atoms, and some device names some value exactly 256 times.
All inputs are finite; a program needn't handle non-finite values.
Results may differ from a plain program's by a relative error of at most 0.0055.
Values may be sent and summed in bfloat16 or wider, within the bound.
No kernel may reach another device: no remote copies, remote signals or barrier semaphores. Data moves between devices by JAX's collectives and lax.ppermute only.
A program may use at most 128 MiB of HBM per device.

v0:
```python
import jax
import jax.numpy as jnp
from jax import lax
from jax.sharding import PartitionSpec as P

BX = 32
GY = 512
GZ = 512


def from_behind(shard, axis, by):
    count = lax.axis_size(axis)
    return lax.ppermute(shard, axis, [(i, (i + by) % count) for i in range(count)])


def bspline(u):
    u2 = u * u
    u3 = u2 * u
    w0 = (1.0 - u) * (1.0 - u) * (1.0 - u) / 6.0
    w1 = (3.0 * u3 - 6.0 * u2 + 4.0) / 6.0
    w2 = (-3.0 * u3 + 3.0 * u2 + 3.0 * u + 1.0) / 6.0
    w3 = u3 / 6.0
    return jnp.stack([w0, w1, w2, w3])


def spline_rows(base, weights, width, wrap):
    columns = jnp.arange(width, dtype=jnp.int32)[None, :]
    total = jnp.zeros((base.shape[0], width), jnp.float32)
    for shift_k in range(4):
        place = base + shift_k
        if wrap:
            place = place % width
        total = total + weights[shift_k][:, None] * (place[:, None] == columns).astype(jnp.float32)
    return total


def dest_rank(target, n_col, block):
    atoms = target.shape[0]
    groups = atoms // block
    onehot = (target[:, None] == jnp.arange(n_col, dtype=jnp.int32)[None, :]).astype(jnp.bfloat16)
    grouped = onehot.reshape(groups, block, n_col)
    lower = (
        jnp.arange(block, dtype=jnp.int32)[:, None] >= jnp.arange(block, dtype=jnp.int32)[None, :]
    ).astype(jnp.bfloat16)
    within = jnp.einsum("ij,gjd->gid", lower, grouped, preferred_element_type=jnp.float32)
    totals = within[:, block - 1, :].astype(jnp.bfloat16)
    before = (
        jnp.arange(groups, dtype=jnp.int32)[:, None] > jnp.arange(groups, dtype=jnp.int32)[None, :]
    ).astype(jnp.bfloat16)
    offsets = jnp.dot(before, totals, preferred_element_type=jnp.float32)
    counted = (within + offsets[:, None, :]) * grouped.astype(jnp.float32)
    rank = jnp.sum(counted, axis=2).reshape(atoms).astype(jnp.int32) - 1
    return onehot, rank


def body(features, position, velocity, noise, charge, frac, cell, dest, w_in, w_out, w_force):
    n_col = lax.axis_size("col")
    row_id = lax.axis_index("row")
    col_id = lax.axis_index("col")
    atoms = features.shape[0]
    width = features.shape[1]
    slots = 2 * atoms // n_col
    target = dest[:, 0]
    onehot, rank = dest_rank(target, n_col, 256)
    hidden = jax.nn.silu(jnp.dot(features, w_in, preferred_element_type=jnp.float32)).astype(
        jnp.bfloat16
    )
    new_feat = (
        features.astype(jnp.float32) + jnp.dot(hidden, w_out, preferred_element_type=jnp.float32)
    ).astype(jnp.bfloat16)
    slot = target * slots + rank
    feat_buf = (
        jnp.zeros((n_col * slots, width), jnp.bfloat16)
        .at[slot]
        .set(new_feat, unique_indices=True, mode="promise_in_bounds")
        .reshape(n_col, slots, width)
    )
    feat_buf, hidden, rank, onehot, charge, frac, cell = lax.optimization_barrier(
        (feat_buf, hidden, rank, onehot, charge, frac, cell)
    )
    got_feat = lax.all_to_all(feat_buf, "col", split_axis=0, concat_axis=0, tiled=True)
    force = lax.dot_general(
        w_force, hidden, (((1,), (1,)), ((), ())), preferred_element_type=jnp.float32
    )
    new_vel = 0.8 * velocity + 0.5 * force + 0.6 * noise
    state = jnp.concatenate([position + 0.5 * new_vel, new_vel], axis=0)
    rank_hot = (rank[:, None] == jnp.arange(slots, dtype=jnp.int32)[None, :]).astype(jnp.bfloat16)
    state_lhs = state.astype(jnp.bfloat16)[:, None, :] * onehot.T[None, :, :]
    state_buf = jnp.dot(
        state_lhs.reshape(6 * n_col, atoms), rank_hot, preferred_element_type=jnp.float32
    ).astype(jnp.bfloat16).reshape(6, n_col, slots)
    planes_z = GZ // n_col
    ext_x = BX + 3
    ext_z = planes_z + 3
    local_x = cell[0] - row_id * BX
    local_y = cell[1]
    local_z = cell[2] - col_id * planes_z
    wx = bspline(frac[0])
    wy = bspline(frac[1])
    wz = bspline(frac[2])
    block = atoms
    extended = jnp.zeros((ext_z * ext_x, GY), jnp.float32)
    for start in range(0, atoms, block):
        stop = start + block
        rows_x = spline_rows(local_x[start:stop], wx[:, start:stop], ext_x, False)
        rows_y = spline_rows(local_y[start:stop], wy[:, start:stop], GY, True)
        rows_z = spline_rows(local_z[start:stop], wz[:, start:stop], ext_z, False)
        kron = (
            charge[start:stop][:, None, None] * rows_z[:, :, None] * rows_x[:, None, :]
        ).reshape(block, ext_z * ext_x)
        extended = extended + lax.dot_general(
            kron,
            rows_y,
            (((0,), (0,)), ((), ())),
            precision=lax.Precision.HIGH,
            preferred_element_type=jnp.float32,
        )
    extended = extended.reshape(ext_z, ext_x, GY)
    from_below = from_behind(extended[:, BX:, :].astype(jnp.bfloat16), "row", 1).astype(jnp.float32)
    slab = extended[:, :BX, :].at[:, :3, :].add(from_below)
    from_lower = from_behind(slab[planes_z:].astype(jnp.bfloat16), "col", 1).astype(jnp.float32)
    brick = slab[:planes_z].at[:3].add(from_lower).astype(jnp.bfloat16)
    brick, got_feat, state_buf = lax.optimization_barrier((brick, got_feat, state_buf))
    arrived_feat = got_feat.reshape(n_col * slots, width)
    y_block = GY // n_col
    state_part = state_buf.transpose(1, 0, 2).reshape(n_col, 6 * slots)
    grid_part = (
        brick.reshape(planes_z, BX, n_col, y_block).transpose(2, 0, 1, 3).reshape(n_col, -1)
    )
    got = lax.all_to_all(
        jnp.concatenate([state_part, grid_part], axis=1), "col", split_axis=0, concat_axis=0, tiled=True
    )
    arrived_state = (
        got[:, : 6 * slots].reshape(n_col, 6, slots).transpose(1, 0, 2).reshape(6, n_col * slots)
    ).astype(jnp.float32)
    pencil = got[:, 6 * slots :].reshape(n_col * planes_z, BX * y_block)
    table = dft_table()
    table_hi = table.astype(jnp.bfloat16)
    table_lo = (table - table_hi.astype(jnp.float32)).astype(jnp.bfloat16)
    dims = (((0,), (0,)), ((), ()))
    both = lax.dot_general(
        pencil, table_hi, dims, preferred_element_type=jnp.float32
    ) + lax.dot_general(pencil, table_lo, dims, preferred_element_type=jnp.float32)
    norm_scale = 1.0 / jnp.sqrt(jnp.float32(GZ))
    both = both.reshape(BX, y_block, 2 * GZ)
    real_part = both[..., :GZ] * norm_scale
    imag_part = -both[..., GZ:] * norm_scale
    spectrum = jnp.stack([real_part, imag_part])
    return (arrived_feat, arrived_state, spectrum)


def dft_table():
    coarse = GZ // 32
    z = jnp.arange(GZ, dtype=jnp.int32)[:, None]
    step = 2.0 * jnp.pi / GZ
    hi_angle = step * ((z * (32 * jnp.arange(coarse, dtype=jnp.int32)[None, :])) % GZ).astype(jnp.float32)
    lo_angle = step * ((z * jnp.arange(32, dtype=jnp.int32)[None, :]) % GZ).astype(jnp.float32)
    ca, sa = jnp.cos(hi_angle)[:, :, None], jnp.sin(hi_angle)[:, :, None]
    cb, sb = jnp.cos(lo_angle)[:, None, :], jnp.sin(lo_angle)[:, None, :]
    cos_t = (ca * cb - sa * sb).reshape(GZ, GZ)
    sin_t = (sa * cb + ca * sb).reshape(GZ, GZ)
    return jnp.concatenate([cos_t, sin_t], axis=1)


def solution(mesh):
    in_specs = (
        P(("row", "col"), None),
        P(None, ("row", "col")),
        P(None, ("row", "col")),
        P(None, ("row", "col")),
        P(("row", "col")),
        P(None, ("row", "col")),
        P(None, ("row", "col")),
        P(("row", "col"), None),
        P(),
        P(),
        P(),
    )
    out_specs = (P(("row", "col"), None), P(None, ("row", "col")), P(None, "row", "col", None))
    return jax.shard_map(body, mesh=mesh, in_specs=in_specs, out_specs=out_specs, check_vma=False)
```

profile of v0, /device:TPU:1, one launch (start us, length us, event | category | flops | bytes accessed | tf_op | source)
XLA Modules:
  0.0 178.1 jit_solution(14961716756569377377)
XLA Ops:
  0.6 0.0 copy-start
  0.6 0.5 broadcast.895
  1.2 1.5 reduce.9
  2.7 0.9 fusion.29
  3.6 0.0 copy-start.5
  3.6 0.0 copy-start.4
  3.6 0.5 fusion.26
  4.1 0.1 convert_bitcast_fusion
  4.3 0.5 slice_reduce_fusion
  4.8 0.1 fusion.91
  4.9 0.7 fusion.24
  5.7 0.1 compare_select_fusion
  5.8 0.0 copy-start.11
  5.8 2.6 %multiply_convert_fusion = bf16[8192,256]{1,0:T(8,128)(2,1)S(1)} fusion(bf16[8192,128]{1,0:T(8,128)(2,1)S(1)} %copy-done.4, bf16[128,256]{1,0:T(8,128)(2,1)S(1)} %copy-done), kind=kOutput, calls=%fused_computation.30 | convolution fusion | flops 547356672 | bytes 6356992 | tf_op jit(solution)/shard_map/dot_general | solution.py:65
  8.4 1.2 fusion.9
  9.7 0.7 copy-done.2
  10.3 23.7 %scatter_custom_fusion = bf16[16384,128]{1,0:T(8,128)(2,1)} fusion(s32[8192]{0:T(1024)S(1)} %bitcast.106, bf16[8192,128]{1,0:T(8,128)(2,1)S(1)} %fusion.9, bf16[]{:T(256)} %constant.149.clone.1), kind=kCustom, calls=%fused_computation.43 | custom fusion | bytes 4194306 | tf_op jit(solution)/shard_map/scatter | solution.py:75
  34.1 13.3 %all-to-all-start = ((bf16[64,256,128]{2,1,0:T(8,128)(2,1)}), bf16[64,256,128]{2,1,0:T(8,128)(2,1)}, u32[]{:S(2)}, u32[]{:S(2)}) async-start(bf16[64,256,128]{2,1,0:T(8,128)(2,1)} %bitcast.82), calls=%async_computation | async-start | bytes 8388608 | tf_op jit(solution)/shard_map/all_to_all | solution.py:81
  47.4 0.1 fusion.95
  47.5 0.1 fusion.96
  47.7 0.5 select_add_fusion
  48.2 0.2 add_multiply_fusion
  48.4 6.9 %broadcast_multiply_fusion = f32[8192,11,35]{0,2,1:T(8,128)} fusion(f32[8192,35]{0,1:T(8,128)S(1)} %select_add_fusion, f32[8192,11]{0,1:T(8,128)S(1)} %add_multiply_fusion), kind=kLoop, calls=%fused_computation.32 | loop fusion | flops 3153920 | bytes 14123008 | tf_op jit(solution)/shard_map/mul | solution.py:109
  55.3 13.1 %mul.612 = f32[8192,385]{0,1:T(8,128)} reshape(f32[8192,11,35]{0,2,1:T(8,128)} %broadcast_multiply_fusion) | data formatting | bytes 25231360 | tf_op jit(solution)/shard_map/mul | solution.py:109
  68.4 13.2 %dot_general.36 = f32[11,35,8192]{2,1,0:T(8,128)} reshape(f32[385,8192]{1,0:T(8,128)} %bitcast.81) | data formatting | bytes 25231360 | tf_op jit(solution)/shard_map/dot_general | solution.py:111
  81.6 0.1 add_select_fusion.5
  81.7 0.0 copy-start.6
  81.7 0.0 copy-start.7
  81.7 0.0 copy-start.8
  81.7 0.0 copy-start.13
  81.8 29.0 %fusion = f32[11,35,512]{2,1,0:T(8,128)S(1)} fusion(f32[11,35,8192]{2,1,0:T(8,128)} %dot_general.36, f32[8192]{0:T(1024)S(1)} %get-tuple-element.65, s32[8192]{0:T(1024)S(1)} %get-tuple-element.62, f32[8192]{0:T(1024)S(1)} %get-tuple-element.64, s32[8192]{0:T(1024)S(1)} %get-tuple-element.61, f32[8192]{0:T(1024)S(1)} %get-tuple-element.66, ...), kind=kOutput, calls=%fused_computation.1 | convolution fusion | flops 9734979584 | bytes 13666304 | tf_op jit(solution)/shard_map/dot_general | solution.py:111
  110.8 1.4 collective-permute-start
  112.2 1.2 add_convert_fusion
  113.4 0.1 pad_maximum_fusion.2
  113.5 3.1 %broadcast_multiply_fusion.1 = bf16[6,64,8192]{2,1,0:T(8,128)(2,1)} fusion(bf16[64,8192]{1,0:T(8,128)(2,1)S(1)} %bitcast.88, bf16[6,8192]{1,0:T(8,128)(2,1)S(1)} %pad_maximum_fusion.2), kind=kLoop, calls=%fused_computation.34 | loop fusion | flops 3145728 | bytes 7438336 | tf_op jit(solution)/shard_map/mul | solution.py:88
  116.6 0.1 slice.116
  116.7 0.0 collective-permute-done
  116.7 0.3 scatter-add.6
  117.1 2.2 %collective-permute-start.1 = (bf16[3,32,512]{2,1,0:T(8,128)(2,1)S(1)}, bf16[3,32,512]{2,1,0:T(8,128)(2,1)S(1)}, u32[]{:S(2)}, u32[]{:S(2)}) collective-permute-start(bf16[3,32,512]{2,1,0:T(8,128)(2,1)S(1)} %slice.144), channel_id=1, source_target_pairs={{0,1},{1,2},{2,3},{3,4},{4,5},{5,6},{6,7},{7,8},{8,9},{9,10},{10,1... | collective-permute-start | bytes 294920 | tf_op jit(solution)/shard_map/ppermute | solution.py:13
  119.3 5.1 %fusion.34 = bf16[384,256]{1,0:T(8,128)(2,1)S(1)} fusion(bf16[384,8192]{1,0:T(8,128)(2,1)} %bitcast.87, s32[8192]{0:T(1024)S(1)} %bitcast.107), kind=kOutput, calls=%fused_computation.55 | convolution fusion | flops 1612808192 | bytes 6520832 | tf_op jit(solution)/shard_map/dot_general | solution.py:89
  124.4 13.4 %collective-permute-done.1 = bf16[3,32,512]{2,1,0:T(8,128)(2,1)S(1)} collective-permute-done((bf16[3,32,512]{2,1,0:T(8,128)(2,1)S(1)}, bf16[3,32,512]{2,1,0:T(8,128)(2,1)S(1)}, u32[]{:S(2)}, u32[]{:S(2)}) %collective-permute-start.1) | collective-permute-done | bytes 98336 | tf_op jit(solution)/shard_map/ppermute | solution.py:13
  137.9 5.8 %all-to-all-done = bf16[64,256,128]{2,1,0:T(8,128)(2,1)} async-done(((bf16[64,256,128]{2,1,0:T(8,128)(2,1)}), bf16[64,256,128]{2,1,0:T(8,128)(2,1)}, u32[]{:S(2)}, u32[]{:S(2)}) %all-to-all-start) | async-done | bytes 4194336 | tf_op jit(solution)/shard_map/all_to_all | solution.py:81
  143.7 0.2 copy.45
  143.9 0.5 copy.41
  144.4 0.7 copy.42
  145.1 0.2 maximum_bitcast_fusion
  145.3 0.5 broadcast.898
  145.8 1.6 reduce.10
  147.4 0.3 copy.52
  147.7 0.9 reshape.820
  148.6 6.2 %all-to-all-start.1 = ((bf16[64,2,1792]{2,1,0:T(2,128)(2,1)}), bf16[64,2,1792]{2,1,0:T(2,128)(2,1)S(1)}, u32[]{:S(2)}, u32[]{:S(2)}) async-start(bf16[64,2,1792]{2,1,0:T(2,128)(2,1)} %reshape.820), calls=%async_computation.1 | async-start | bytes 917504 | tf_op jit(solution)/shard_map/all_to_all | solution.py:130
  154.8 0.3 fusion.79
  155.0 0.2 fusion.90
  155.3 0.3 multiply_subtract_fusion
  155.6 15.1 %all-to-all-done.1 = bf16[64,2,1792]{2,1,0:T(2,128)(2,1)S(1)} async-done(((bf16[64,2,1792]{2,1,0:T(2,128)(2,1)}), bf16[64,2,1792]{2,1,0:T(2,128)(2,1)S(1)}, u32[]{:S(2)}, u32[]{:S(2)}) %all-to-all-start.1) | async-done | bytes 458784 | tf_op jit(solution)/shard_map/all_to_all | solution.py:130
  170.6 0.4 reshape.821
  171.0 0.1 copy.51
  171.1 0.1 reshape.794
  171.3 0.9 reshape.797
  172.2 0.5 fusion.32
  172.7 0.5 fusion.31
  173.2 0.1 fusion.38
  173.3 1.0 pad_maximum_fusion.1
  174.3 3.8 %copy.56 = bf16[16384,128]{1,0:T(8,128)(2,1)} copy(bf16[16384,128]{1,0:T(8,128)(2,1)} %bitcast.18) | data formatting | bytes 8388608
  (36 shorter events, 0.4 us)
Async XLA Ops:
  0.6 5.2 %copy-start = (bf16[128,256]{1,0:T(8,128)(2,1)S(1)}, bf16[128,256]{1,0:T(8,128)(2,1)}, u32[]{:S(2)}) copy-start(bf16[128,256]{1,0:T(8,128)(2,1)} %param.23) | copy-start | bytes 196612
  3.6 2.1 %copy-start.5 = (s32[8192,1]{0,1:T(1,128)S(1)}, s32[8192,1]{0,1:T(1,128)}, u32[]{:S(2)}) copy-start(s32[8192,1]{0,1:T(1,128)} %param.22) | copy-start | bytes 98308
  3.6 2.2 %copy-start.4 = (bf16[8192,128]{1,0:T(8,128)(2,1)S(1)}, bf16[8192,128]{1,0:T(8,128)(2,1)}, u32[]{:S(2)}) copy-start(bf16[8192,128]{1,0:T(8,128)(2,1)} %param.15) | copy-start | bytes 6291460
  5.8 2.6 %copy-start.11 = (bf16[256,128]{1,0:T(8,128)(2,1)S(1)}, bf16[256,128]{1,0:T(8,128)(2,1)}, u32[]{:S(2)}) copy-start(bf16[256,128]{1,0:T(8,128)(2,1)} %param.24) | copy-start | bytes 196612
  8.4 1.9 %copy-start.2 = (bf16[8192,256]{1,0:T(8,128)(2,1)}, bf16[8192,256]{1,0:T(8,128)(2,1)S(1)}, u32[]{:S(2)}) copy-start(bf16[8192,256]{1,0:T(8,128)(2,1)S(1)} %multiply_convert_fusion) | copy-start | bytes 12582916
  34.1 13.3 %copy-start.9 = (s32[3,8192]{1,0:T(4,128)S(1)}, s32[3,8192]{1,0:T(4,128)}, u32[]{:S(2)}) copy-start(s32[3,8192]{1,0:T(4,128)} %param.21) | copy-start | bytes 294916
  34.1 13.4 %copy-start.10 = (f32[3,8192]{1,0:T(4,128)S(1)}, f32[3,8192]{1,0:T(4,128)}, u32[]{:S(2)}) copy-start(f32[3,8192]{1,0:T(4,128)} %param.20) | copy-start | bytes 294916
  34.1 14.1 %copy-start.12 = (f32[8192]{0:T(1024)S(1)}, f32[8192]{0:T(1024)}, u32[]{:S(2)}) copy-start(f32[8192]{0:T(1024)} %param.19) | copy-start | bytes 98308
  34.1 109.6 %all-to-all-start = ((bf16[64,256,128]{2,1,0:T(8,128)(2,1)}), bf16[64,256,128]{2,1,0:T(8,128)(2,1)}, u32[]{:S(2)}, u32[]{:S(2)}) async-start(bf16[64,256,128]{2,1,0:T(8,128)(2,1)} %bitcast.82), calls=%async_computation | async-start | bytes 8388608 | tf_op jit(solution)/shard_map/all_to_all | solution.py:81
  81.7 30.5 %copy-start.3 = (bf16[8192,256]{1,0:T(8,128)(2,1)S(1)}, bf16[8192,256]{1,0:T(8,128)(2,1)}, u32[]{:S(2)}) copy-start(bf16[8192,256]{1,0:T(8,128)(2,1)} %copy-done.2) | copy-start | bytes 12582916
  81.7 30.5 %copy-start.6 = (f32[3,8192]{1,0:T(4,128)S(1)}, f32[3,8192]{1,0:T(4,128)}, u32[]{:S(2)}) copy-start(f32[3,8192]{1,0:T(4,128)} %param.16) | copy-start | bytes 294916
  81.7 30.5 %copy-start.7 = (f32[3,8192]{1,0:T(4,128)S(1)}, f32[3,8192]{1,0:T(4,128)}, u32[]{:S(2)}) copy-start(f32[3,8192]{1,0:T(4,128)} %param.18) | copy-start | bytes 294916
  81.7 30.5 %copy-start.8 = (f32[3,8192]{1,0:T(4,128)S(1)}, f32[3,8192]{1,0:T(4,128)}, u32[]{:S(2)}) copy-start(f32[3,8192]{1,0:T(4,128)} %param.17) | copy-start | bytes 294916
  81.7 30.5 %copy-start.13 = (bf16[3,256]{1,0:T(4,128)(2,1)S(1)}, bf16[3,256]{1,0:T(4,128)(2,1)}, u32[]{:S(2)}) copy-start(bf16[3,256]{1,0:T(4,128)(2,1)} %param.25) | copy-start | bytes 4612
  110.8 5.9 %collective-permute-start = (bf16[11,3,512]{2,1,0:T(4,128)(2,1)S(1)}, bf16[11,3,512]{2,1,0:T(4,128)(2,1)S(1)}, u32[]{:S(2)}, u32[]{:S(2)}) collective-permute-start(bf16[11,3,512]{2,1,0:T(4,128)(2,1)S(1)} %slice.145), channel_id=1, source_target_pairs={{0,64},{64,128},{128,192},{192,0},{1,65},{65,129},{129,193},{193,1... | collective-permute-start | bytes 101384 | tf_op jit(solution)/shard_map/ppermute | solution.py:13
  117.1 20.7 %collective-permute-start.1 = (bf16[3,32,512]{2,1,0:T(8,128)(2,1)S(1)}, bf16[3,32,512]{2,1,0:T(8,128)(2,1)S(1)}, u32[]{:S(2)}, u32[]{:S(2)}) collective-permute-start(bf16[3,32,512]{2,1,0:T(8,128)(2,1)S(1)} %slice.144), channel_id=1, source_target_pairs={{0,1},{1,2},{2,3},{3,4},{4,5},{5,6},{6,7},{7,8},{8,9},{9,10},{10,1... | collective-permute-start | bytes 294920 | tf_op jit(solution)/shard_map/ppermute | solution.py:13
  148.6 22.1 %all-to-all-start.1 = ((bf16[64,2,1792]{2,1,0:T(2,128)(2,1)}), bf16[64,2,1792]{2,1,0:T(2,128)(2,1)S(1)}, u32[]{:S(2)}, u32[]{:S(2)}) async-start(bf16[64,2,1792]{2,1,0:T(2,128)(2,1)} %reshape.820), calls=%async_computation.1 | async-start | bytes 917504 | tf_op jit(solution)/shard_map/all_to_all | solution.py:130
  174.3 3.8 %copy-start.1 = (bf16[128,256]{1,0:T(8,128)(2,1)S(1)}, bf16[128,256]{1,0:T(8,128)(2,1)}, u32[]{:S(2)}) copy-start(bf16[128,256]{1,0:T(8,128)(2,1)} %param.23) | copy-start | bytes 196612
where the time goes:
time: 179 us; the launch traced here: 178 us
  local copies, waits for them, and re-layouts  60.8 us (34%)
  matrix products  40.7 us (23%)
  waiting for transfers between devices  34.3 us (19%)
  starting transfers between devices  23.1 us (13%)
  other arithmetic  18 us (10%)
    dot_general x1, matrix products, body(): lax.dot_general(kron, rows_y, (((0,), (0,)), ((), ())), precision=lax.Pre...  29 us
    scatter x1, local copies, waits for them, and re-layouts, body(): feat_buf = jnp.zeros((n_col * slots, width), jnp.bfloat16).at[slot].set(n...  23.7 us
    all_to_all x1, waiting for transfers between devices, body(): lax.all_to_all(jnp.concatenate([state_part, grid_part], axis=1), 'col', s...  15.1 us
    ppermute x2, waiting for transfers between devices, from_behind(): lax.ppermute(shard, axis, [(i, (i + by) % count) for i in range(count)])  13.4 us
    all_to_all x1, starting transfers between devices, body(): lax.all_to_all(feat_buf, 'col', split_axis=0, concat_axis=0, tiled=True)  13.3 us
    dot_general x1, local copies, waits for them, and re-layouts, body(): lax.dot_general(kron, rows_y, (((0,), (0,)), ((), ())), precision=lax.Pre...  13.2 us
    mul x1, local copies, waits for them, and re-layouts, body(): charge[start:stop][:, None, None] * rows_z[:, :, None] * rows_x[:, None, :]  13.1 us
    mul x2, other arithmetic, body(): charge[start:stop][:, None, None] * rows_z[:, :, None] * rows_x[:, None, :]  7.08 us
  transfers between devices with their start and end apart: 4, of which 3 were waited for; matrix products, arithmetic and copies ran while one was open for 42% of the time, Pallas kernels for 0%

commit v1 on v0

--- a/solution.py
+++ b/solution.py
@@ -53,6 +53,10 @@
     return onehot, rank
 
 
+def feature_hidden(feat, w_in):
+    return jax.nn.silu(jnp.dot(feat, w_in, preferred_element_type=jnp.float32)).astype(jnp.bfloat16)
+
+
 def body(features, position, velocity, noise, charge, frac, cell, dest, w_in, w_out, w_force):
     n_col = lax.axis_size("col")
     row_id = lax.axis_index("row")
@@ -62,23 +66,18 @@
     slots = 2 * atoms // n_col
     target = dest[:, 0]
     onehot, rank = dest_rank(target, n_col, 256)
-    hidden = jax.nn.silu(jnp.dot(features, w_in, preferred_element_type=jnp.float32)).astype(
-        jnp.bfloat16
-    )
-    new_feat = (
-        features.astype(jnp.float32) + jnp.dot(hidden, w_out, preferred_element_type=jnp.float32)
-    ).astype(jnp.bfloat16)
     slot = target * slots + rank
     feat_buf = (
         jnp.zeros((n_col * slots, width), jnp.bfloat16)
         .at[slot]
-        .set(new_feat, unique_indices=True, mode="promise_in_bounds")
+        .set(features, unique_indices=True, mode="promise_in_bounds")
         .reshape(n_col, slots, width)
     )
-    feat_buf, hidden, rank, onehot, charge, frac, cell = lax.optimization_barrier(
-        (feat_buf, hidden, rank, onehot, charge, frac, cell)
+    feat_buf, features, rank, onehot, charge, frac, cell = lax.optimization_barrier(
+        (feat_buf, features, rank, onehot, charge, frac, cell)
     )
     got_feat = lax.all_to_all(feat_buf, "col", split_axis=0, concat_axis=0, tiled=True)
+    hidden = feature_hidden(features, w_in)
     force = lax.dot_general(
         w_force, hidden, (((1,), (1,)), ((), ())), preferred_element_type=jnp.float32
     )
@@ -120,16 +119,20 @@
     slab = extended[:, :BX, :].at[:, :3, :].add(from_below)
     from_lower = from_behind(slab[planes_z:].astype(jnp.bfloat16), "col", 1).astype(jnp.float32)
     brick = slab[:planes_z].at[:3].add(from_lower).astype(jnp.bfloat16)
-    brick, got_feat, state_buf = lax.optimization_barrier((brick, got_feat, state_buf))
-    arrived_feat = got_feat.reshape(n_col * slots, width)
     y_block = GY // n_col
     state_part = state_buf.transpose(1, 0, 2).reshape(n_col, 6 * slots)
     grid_part = (
         brick.reshape(planes_z, BX, n_col, y_block).transpose(2, 0, 1, 3).reshape(n_col, -1)
     )
-    got = lax.all_to_all(
-        jnp.concatenate([state_part, grid_part], axis=1), "col", split_axis=0, concat_axis=0, tiled=True
-    )
+    send = jnp.concatenate([state_part, grid_part], axis=1)
+    send, got_feat = lax.optimization_barrier((send, got_feat))
+    got = lax.all_to_all(send, "col", split_axis=0, concat_axis=0, tiled=True)
+    arrived = got_feat.reshape(n_col * slots, width)
+    arrived_hidden = feature_hidden(arrived, w_in)
+    arrived_feat = (
+        arrived.astype(jnp.float32)
+        + jnp.dot(arrived_hidden, w_out, preferred_element_type=jnp.float32)
+    ).astype(jnp.bfloat16)
     arrived_state = (
         got[:, : 6 * slots].reshape(n_col, 6, slots).transpose(1, 0, 2).reshape(6, n_col * slots)
     ).astype(jnp.float32)

time: 179 us -> 174 us (0.972)
  waiting for transfers between devices: 34.3 us -> 21.9 us
  matrix products: 40.7 us -> 46.2 us
  starting transfers between devices: 23.1 us -> 27.3 us
    all_to_all x1, waiting for transfers between devices: 15.1 us -> 6.47 us  [body(): got = lax.all_to_all(send, 'col', split_axis=0, concat_axis=0, tiled=True)]
    dot_general x2 -> x1, matrix products: 3.82 us -> 9.41 us  [body(): jnp.dot(arrived_hidden, w_out, preferred_element_type=jnp.float32)]
    all_to_all x1, waiting for transfers between devices: 5.83 us -> 1.47 us  [body(): lax.all_to_all(feat_buf, 'col', split_axis=0, concat_axis=0, tiled=True)]
    all_to_all x1, starting transfers between devices: 6.17 us -> 10.5 us  [body(): got = lax.all_to_all(send, 'col', split_axis=0, concat_axis=0, tiled=True)]
    unnamed x36 -> x25, local copies, waits for them, and re-layouts: 6.67 us -> 3.37 us
    dot_general x1, matrix products: 5.09 us -> 2.23 us  [body(): jnp.dot(state_lhs.reshape(6 * n_col, atoms), rank_hot, preferred_element_...]
    dot_general x1, matrix products: 1.19 us -> 4.04 us  [body(): lax.dot_general(w_force, hidden, (((1,), (1,)), ((), ())), preferred_elem...]
    mul x1, other arithmetic: 3.13 us -> 0.46 us  [body(): state_lhs = state.astype(jnp.bfloat16)[:, None, :] * onehot.T[None, :, :]]
  transfers between devices with their start and end apart: 4 -> 4, of which waited for: 3 -> 3; matrix products, arithmetic and copies ran while one was open for 42% -> 50% of each run, Pallas kernels for 0% -> 0%
where the time goes in v1:
time: 174 us
  local copies, waits for them, and re-layouts  59.9 us (34%)
  matrix products  46.2 us (27%)
  starting transfers between devices  27.3 us (16%)
  waiting for transfers between devices  21.9 us (13%)
  other arithmetic  17.2 us (10%)
    dot_general x1, matrix products, body(): lax.dot_general(kron, rows_y, (((0,), (0,)), ((), ())), precision=lax.Pre...  29 us
    scatter x1, local copies, waits for them, and re-layouts, body(): feat_buf = jnp.zeros((n_col * slots, width), jnp.bfloat16).at[slot].set(f...  24 us
    ppermute x2, waiting for transfers between devices, from_behind(): lax.ppermute(shard, axis, [(i, (i + by) % count) for i in range(count)])  14 us
    all_to_all x1, starting transfers between devices, body(): lax.all_to_all(feat_buf, 'col', split_axis=0, concat_axis=0, tiled=True)  13.3 us
    dot_general x1, local copies, waits for them, and re-layouts, body(): lax.dot_general(kron, rows_y, (((0,), (0,)), ((), ())), precision=lax.Pre...  13.2 us
    mul x1, local copies, waits for them, and re-layouts, body(): charge[start:stop][:, None, None] * rows_z[:, :, None] * rows_x[:, None, :]  13.1 us
    all_to_all x1, starting transfers between devices, body(): got = lax.all_to_all(send, 'col', split_axis=0, concat_axis=0, tiled=True)  10.5 us
    dot_general x1, matrix products, body(): jnp.dot(arrived_hidden, w_out, preferred_element_type=jnp.float32)  9.41 us
  transfers between devices with their start and end apart: 4, of which 3 were waited for; matrix products, arithmetic and copies ran while one was open for 50% of the time, Pallas kernels for 0%

profile of v1, /device:TPU:1, one launch (start us, length us, event | category | flops | bytes accessed | tf_op | source)
XLA Modules:
  0.0 173.7 jit_solution(8117570033285875848)
XLA Ops:
  0.6 0.0 copy-start
  0.6 0.0 copy-start.1
  0.7 0.5 broadcast.897
  1.2 1.5 reduce.9
  2.7 0.5 fusion.26
  3.2 0.1 convert_bitcast_fusion
  3.3 0.5 slice_reduce_fusion
  3.9 0.1 fusion.91
  4.0 0.7 fusion.24
  4.7 0.0 copy-done.1
  4.7 0.1 compare_select_fusion
  4.8 0.2 fusion.29
  5.0 24.0 %scatter_custom_fusion = bf16[16384,128]{1,0:T(8,128)(2,1)} fusion(s32[8192]{0:T(1024)S(1)} %bitcast.106, bf16[8192,128]{1,0:T(8,128)(2,1)} %param.15, bf16[]{:T(256)} %constant.152.clone.1), kind=kCustom, calls=%fused_computation.44 | custom fusion | bytes 4194816 | tf_op jit(solution)/shard_map/scatter | solution.py:73
  29.0 13.3 %all-to-all-start = ((bf16[64,256,128]{2,1,0:T(8,128)(2,1)}), bf16[64,256,128]{2,1,0:T(8,128)(2,1)}, u32[]{:S(2)}, u32[]{:S(2)}) async-start(bf16[64,256,128]{2,1,0:T(8,128)(2,1)} %bitcast.81), calls=%async_computation | async-start | bytes 8388608 | tf_op jit(solution)/shard_map/all_to_all | solution.py:79
  42.3 0.0 copy-done.2
  42.3 0.1 fusion.97
  42.4 0.0 copy-done.3
  42.4 0.1 fusion.98
  42.6 0.5 select_add_fusion
  43.1 0.2 add_multiply_fusion
  43.3 6.9 %broadcast_multiply_fusion = f32[8192,11,35]{0,2,1:T(8,128)} fusion(f32[8192,35]{0,1:T(8,128)S(1)} %select_add_fusion, f32[8192,11]{0,1:T(8,128)S(1)} %add_multiply_fusion), kind=kLoop, calls=%fused_computation.33 | loop fusion | flops 3153920 | bytes 14123008 | tf_op jit(solution)/shard_map/mul | solution.py:108
  50.2 13.1 %mul.627 = f32[8192,385]{0,1:T(8,128)} reshape(f32[8192,11,35]{0,2,1:T(8,128)} %broadcast_multiply_fusion) | data formatting | bytes 25231360 | tf_op jit(solution)/shard_map/mul | solution.py:108
  63.3 13.2 %dot_general.40 = f32[11,35,8192]{2,1,0:T(8,128)} reshape(f32[385,8192]{1,0:T(8,128)} %bitcast.80) | data formatting | bytes 25231360 | tf_op jit(solution)/shard_map/dot_general | solution.py:110
  76.5 0.1 add_select_fusion.5
  76.6 0.0 copy-start.5
  76.6 0.0 copy-start.6
  76.6 0.0 copy-start.7
  76.7 0.0 copy-start.8
  76.7 29.0 %fusion.1 = f32[11,35,512]{2,1,0:T(8,128)S(1)} fusion(f32[11,35,8192]{2,1,0:T(8,128)} %dot_general.40, f32[8192]{0:T(1024)S(1)} %get-tuple-element.63, s32[8192]{0:T(1024)S(1)} %get-tuple-element.60, f32[8192]{0:T(1024)S(1)} %get-tuple-element.62, s32[8192]{0:T(1024)S(1)} %get-tuple-element.59, f32[8192]{0:T(1024)S(1)} %get-tuple-element.64, ...), kind=kOutput, calls=%fused_computation.3 | convolution fusion | flops 9734979584 | bytes 13666304 | tf_op jit(solution)/shard_map/dot_general | solution.py:110
  105.7 1.7 collective-permute-start
  107.4 0.2 fusion.90
  107.6 4.0 %add_convert_fusion = (bf16[3,8192]{1,0:T(4,128)(2,1)S(1)}, bf16[3,8192]{1,0:T(4,128)(2,1)S(1)}) fusion(f32[3,8192]{1,0:T(4,128)S(1)} %copy-done.5, f32[3,8192]{1,0:T(4,128)S(1)} %copy-done.6, bf16[3,256]{1,0:T(4,128)(2,1)S(1)} %copy-done.8, bf16[8192,128]{1,0:T(8,128)(2,1)} %param.15, bf16[128,256]{1,0:T(8,128)(2,1)S(1)} %copy-done, ...), kind=kOutput, calls=%fused_computation.83 | convolution fusion | flops 560160768 | bytes 2557440 | tf_op jit(solution)/shard_map/dot_general | solution.py:81
  111.7 0.1 pad_maximum_fusion.3
  111.8 0.5 broadcast_multiply_fusion.1
  112.2 2.2 %fusion.34 = bf16[384,256]{1,0:T(8,128)(2,1)S(1)} fusion(bf16[384,8192]{1,0:T(8,128)(2,1)S(1)} %bitcast.86, s32[8192]{0:T(1024)S(1)} %bitcast.107), kind=kOutput, calls=%fused_computation.56 | convolution fusion | flops 1612808192 | bytes 6520832 | tf_op jit(solution)/shard_map/dot_general | solution.py:88
  114.5 0.3 fusion.79
  114.8 0.1 slice.116
  114.8 0.0 collective-permute-done
  114.9 0.3 scatter-add.6
  115.2 0.7 slice.144
  115.9 1.8 %collective-permute-start.1 = (bf16[3,32,512]{2,1,0:T(8,128)(2,1)}, bf16[3,32,512]{2,1,0:T(8,128)(2,1)}, u32[]{:S(2)}, u32[]{:S(2)}) collective-permute-start(bf16[3,32,512]{2,1,0:T(8,128)(2,1)} %slice.144), channel_id=1, source_target_pairs={{0,1},{1,2},{2,3},{3,4},{4,5},{5,6},{6,7},{7,8},{8,9},{9,10},{10,1... | collective-permute-start | bytes 294920 | tf_op jit(solution)/shard_map/ppermute | solution.py:13
  117.7 0.3 multiply_subtract_fusion
  118.0 0.9 copy.45
  119.0 14.0 %collective-permute-done.1 = bf16[3,32,512]{2,1,0:T(8,128)(2,1)} collective-permute-done((bf16[3,32,512]{2,1,0:T(8,128)(2,1)}, bf16[3,32,512]{2,1,0:T(8,128)(2,1)}, u32[]{:S(2)}, u32[]{:S(2)}) %collective-permute-start.1) | collective-permute-done | bytes 98336 | tf_op jit(solution)/shard_map/ppermute | solution.py:13
  132.9 0.9 fusion.41
  133.8 0.5 copy.41
  134.3 1.5 copy.42
  135.8 1.3 pad_maximum_fusion.2
  137.2 1.5 all-to-all-done
  138.6 0.5 broadcast.900
  139.1 2.1 %reduce.10 = bf16[64,3584]{0,1:T(8,128)(2,1)} reduce(bf16[64,1,3584]{0,2,1:T(8,128)(2,1)S(1)} %bitcast.89, bf16[]{:T(256)} %broadcast.900), dimensions={1}, to_apply=%copy.44.reduce_sub_computation | reduce | bytes 917506 | tf_op jit(solution)/shard_map/all_to_all | solution.py:129
  141.2 1.5 copy.52
  142.7 0.9 reshape.820
  143.6 10.5 %all-to-all-start.1 = ((bf16[64,2,1792]{2,1,0:T(2,128)(2,1)}), bf16[64,2,1792]{2,1,0:T(2,128)(2,1)S(1)}, u32[]{:S(2)}, u32[]{:S(2)}) async-start(bf16[64,2,1792]{2,1,0:T(2,128)(2,1)} %reshape.820), calls=%async_computation.1 | async-start | bytes 917504 | tf_op jit(solution)/shard_map/all_to_all | solution.py:129
  154.1 9.4 %fusion = bf16[16384,128]{1,0:T(8,128)(2,1)} fusion(bf16[256,128]{1,0:T(8,128)(2,1)} %param.24, bf16[16384,128]{1,0:T(8,128)(2,1)} %bitcast.23, bf16[128,256]{1,0:T(8,128)(2,1)S(1)} %copy-done), kind=kOutput, calls=%fused_computation.2 | convolution fusion | flops 2174746624 | bytes 8519680 | tf_op jit(solution)/shard_map/dot_general | solution.py:134
  163.5 6.5 %all-to-all-done.1 = bf16[64,2,1792]{2,1,0:T(2,128)(2,1)S(1)} async-done(((bf16[64,2,1792]{2,1,0:T(2,128)(2,1)}), bf16[64,2,1792]{2,1,0:T(2,128)(2,1)S(1)}, u32[]{:S(2)}, u32[]{:S(2)}) %all-to-all-start.1) | async-done | bytes 458784 | tf_op jit(solution)/shard_map/all_to_all | solution.py:129
  170.0 0.4 reshape.821
  170.3 0.1 copy.51
  170.5 0.1 reshape.794
  170.6 0.5 fusion.32
  171.1 0.5 fusion.31
  171.6 0.1 fusion.38
  171.7 0.9 reshape.797
  172.6 1.0 pad_maximum_fusion.1
  (24 shorter events, 0.3 us)
Async XLA Ops:
  0.6 107.0 %copy-start = (bf16[128,256]{1,0:T(8,128)(2,1)S(1)}, bf16[128,256]{1,0:T(8,128)(2,1)}, u32[]{:S(2)}) copy-start(bf16[128,256]{1,0:T(8,128)(2,1)} %param.23) | copy-start | bytes 196612
  0.6 4.1 %copy-start.1 = (s32[8192,1]{0,1:T(1,128)S(1)}, s32[8192,1]{0,1:T(1,128)}, u32[]{:S(2)}) copy-start(s32[8192,1]{0,1:T(1,128)} %param.22) | copy-start | bytes 98308
  29.0 13.3 %copy-start.2 = (s32[3,8192]{1,0:T(4,128)S(1)}, s32[3,8192]{1,0:T(4,128)}, u32[]{:S(2)}) copy-start(s32[3,8192]{1,0:T(4,128)} %param.21) | copy-start | bytes 294916
  29.0 13.4 %copy-start.3 = (f32[3,8192]{1,0:T(4,128)S(1)}, f32[3,8192]{1,0:T(4,128)}, u32[]{:S(2)}) copy-start(f32[3,8192]{1,0:T(4,128)} %param.20) | copy-start | bytes 294916
  29.0 14.1 %copy-start.4 = (f32[8192]{0:T(1024)S(1)}, f32[8192]{0:T(1024)}, u32[]{:S(2)}) copy-start(f32[8192]{0:T(1024)} %param.19) | copy-start | bytes 98308
  29.0 109.6 %all-to-all-start = ((bf16[64,256,128]{2,1,0:T(8,128)(2,1)}), bf16[64,256,128]{2,1,0:T(8,128)(2,1)}, u32[]{:S(2)}, u32[]{:S(2)}) async-start(bf16[64,256,128]{2,1,0:T(8,128)(2,1)} %bitcast.81), calls=%async_computation | async-start | bytes 8388608 | tf_op jit(solution)/shard_map/all_to_all | solution.py:79
  76.6 31.0 %copy-start.5 = (f32[3,8192]{1,0:T(4,128)S(1)}, f32[3,8192]{1,0:T(4,128)}, u32[]{:S(2)}) copy-start(f32[3,8192]{1,0:T(4,128)} %param.16) | copy-start | bytes 294916
  76.6 31.0 %copy-start.6 = (f32[3,8192]{1,0:T(4,128)S(1)}, f32[3,8192]{1,0:T(4,128)}, u32[]{:S(2)}) copy-start(f32[3,8192]{1,0:T(4,128)} %param.18) | copy-start | bytes 294916
  76.6 31.0 %copy-start.7 = (f32[3,8192]{1,0:T(4,128)S(1)}, f32[3,8192]{1,0:T(4,128)}, u32[]{:S(2)}) copy-start(f32[3,8192]{1,0:T(4,128)} %param.17) | copy-start | bytes 294916
  76.7 31.0 %copy-start.8 = (bf16[3,256]{1,0:T(4,128)(2,1)S(1)}, bf16[3,256]{1,0:T(4,128)(2,1)}, u32[]{:S(2)}) copy-start(bf16[3,256]{1,0:T(4,128)(2,1)} %param.25) | copy-start | bytes 4612
  105.7 9.1 %collective-permute-start = (bf16[11,3,512]{2,1,0:T(4,128)(2,1)S(1)}, bf16[11,3,512]{2,1,0:T(4,128)(2,1)S(1)}, u32[]{:S(2)}, u32[]{:S(2)}) collective-permute-start(bf16[11,3,512]{2,1,0:T(4,128)(2,1)S(1)} %slice.145), channel_id=1, source_target_pairs={{0,64},{64,128},{128,192},{192,0},{1,65},{65,129},{129,193},{193,1... | collective-permute-start | bytes 101384 | tf_op jit(solution)/shard_map/ppermute | solution.py:13
  115.9 17.0 %collective-permute-start.1 = (bf16[3,32,512]{2,1,0:T(8,128)(2,1)}, bf16[3,32,512]{2,1,0:T(8,128)(2,1)}, u32[]{:S(2)}, u32[]{:S(2)}) collective-permute-start(bf16[3,32,512]{2,1,0:T(8,128)(2,1)} %slice.144), channel_id=1, source_target_pairs={{0,1},{1,2},{2,3},{3,4},{4,5},{5,6},{6,7},{7,8},{8,9},{9,10},{10,1... | collective-permute-start | bytes 294920 | tf_op jit(solution)/shard_map/ppermute | solution.py:13
  143.6 26.4 %all-to-all-start.1 = ((bf16[64,2,1792]{2,1,0:T(2,128)(2,1)}), bf16[64,2,1792]{2,1,0:T(2,128)(2,1)S(1)}, u32[]{:S(2)}, u32[]{:S(2)}) async-start(bf16[64,2,1792]{2,1,0:T(2,128)(2,1)} %reshape.820), calls=%async_computation.1 | async-start | bytes 917504 | tf_op jit(solution)/shard_map/all_to_all | solution.py:129

commit v2 on v1

--- a/solution.py
+++ b/solution.py
@@ -117,12 +117,11 @@
     extended = extended.reshape(ext_z, ext_x, GY)
     from_below = from_behind(extended[:, BX:, :].astype(jnp.bfloat16), "row", 1).astype(jnp.float32)
     slab = extended[:, :BX, :].at[:, :3, :].add(from_below)
-    from_lower = from_behind(slab[planes_z:].astype(jnp.bfloat16), "col", 1).astype(jnp.float32)
-    brick = slab[:planes_z].at[:3].add(from_lower).astype(jnp.bfloat16)
+    brick = slab.astype(jnp.bfloat16)
     y_block = GY // n_col
     state_part = state_buf.transpose(1, 0, 2).reshape(n_col, 6 * slots)
     grid_part = (
-        brick.reshape(planes_z, BX, n_col, y_block).transpose(2, 0, 1, 3).reshape(n_col, -1)
+        brick.reshape(ext_z, BX, n_col, y_block).transpose(2, 0, 1, 3).reshape(n_col, -1)
     )
     send = jnp.concatenate([state_part, grid_part], axis=1)
     send, got_feat = lax.optimization_barrier((send, got_feat))
@@ -136,7 +135,11 @@
     arrived_state = (
         got[:, : 6 * slots].reshape(n_col, 6, slots).transpose(1, 0, 2).reshape(6, n_col * slots)
     ).astype(jnp.float32)
-    pencil = got[:, 6 * slots :].reshape(n_col * planes_z, BX * y_block)
+    planes = got[:, 6 * slots :].reshape(n_col, ext_z, BX * y_block).astype(jnp.float32)
+    spill = jnp.roll(planes[:, planes_z:], 1, axis=0)
+    pencil = (
+        planes[:, :planes_z].at[:, :3].add(spill).astype(jnp.bfloat16).reshape(GZ, BX * y_block)
+    )
     table = dft_table()
     table_hi = table.astype(jnp.bfloat16)
     table_lo = (table - table_hi.astype(jnp.float32)).astype(jnp.bfloat16)

time: 174 us -> 184 us (1.057)
  local copies, waits for them, and re-layouts: 59.9 us -> 70.8 us
  starting transfers between devices: 27.3 us -> 20.8 us
  other arithmetic: 17.2 us -> 19.9 us
    ppermute x2 -> x1, waiting for transfers between devices: 14 us -> 0.01 us  [from_behind(): lax.ppermute(shard, axis, [(i, (i + by) % count) for i in range(count)])]
    all_to_all x1, waiting for transfers between devices: 1.47 us -> 14.5 us  [body(): lax.all_to_all(feat_buf, 'col', split_axis=0, concat_axis=0, tiled=True)]
    all_to_all x1, starting transfers between devices: 10.5 us -> 5.92 us  [body(): got = lax.all_to_all(send, 'col', split_axis=0, concat_axis=0, tiled=True)]
    unnamed x25 -> x31, local copies, waits for them, and re-layouts: 3.37 us -> 7.68 us
    scatter-add x0 -> x1, local copies, waits for them, and re-layouts: none -> 2.84 us  [body(): planes[:, :planes_z].at[:, :3].add(spill).astype(jnp.bfloat16)]
    convert_element_type x1 -> x2, local copies, waits for them, and re-layouts: 0.48 us -> 2.77 us  [the longest x1 1.47 us: body(): brick = slab.astype(jnp.bfloat16)]
    all_to_all x1, waiting for transfers between devices: 6.47 us -> 8.49 us  [body(): got = lax.all_to_all(send, 'col', split_axis=0, concat_axis=0, tiled=True)]
    ppermute x2 -> x1, starting transfers between devices: 3.52 us -> 1.6 us  [from_behind(): lax.ppermute(shard, axis, [(i, (i + by) % count) for i in range(count)])]
  transfers between devices with their start and end apart: 4 -> 3, of which waited for: 3 -> 2; matrix products, arithmetic and copies ran while one was open for 50% -> 49% of each run, Pallas kernels for 0% -> 0%
where the time goes in v2:
time: 184 us; the launch traced here: 183 us
  local copies, waits for them, and re-layouts  70.8 us (38%)
  matrix products  47 us (26%)
  waiting for transfers between devices  23 us (12%)
  starting transfers between devices  20.8 us (11%)
  other arithmetic  19.9 us (11%)
    dot_general x1, matrix products, body(): lax.dot_general(kron, rows_y, (((0,), (0,)), ((), ())), precision=lax.Pre...  29 us
    scatter x1, local copies, waits for them, and re-layouts, body(): feat_buf = jnp.zeros((n_col * slots, width), jnp.bfloat16).at[slot].set(f...  24 us
    all_to_all x1, waiting for transfers between devices, body(): lax.all_to_all(feat_buf, 'col', split_axis=0, concat_axis=0, tiled=True)  14.5 us
    all_to_all x1, starting transfers between devices, body(): lax.all_to_all(feat_buf, 'col', split_axis=0, concat_axis=0, tiled=True)  13.3 us
    dot_general x1, local copies, waits for them, and re-layouts, body(): lax.dot_general(kron, rows_y, (((0,), (0,)), ((), ())), precision=lax.Pre...  13.2 us
    mul x1, local copies, waits for them, and re-layouts, body(): charge[start:stop][:, None, None] * rows_z[:, :, None] * rows_x[:, None, :]  13.1 us
    dot_general x1, matrix products, body(): jnp.dot(arrived_hidden, w_out, preferred_element_type=jnp.float32)  9.47 us
    all_to_all x1, waiting for transfers between devices, body(): got = lax.all_to_all(send, 'col', split_axis=0, concat_axis=0, tiled=True)  8.49 us
  transfers between devices with their start and end apart: 3, of which 2 were waited for; matrix products, arithmetic and copies ran while one was open for 49% of the time, Pallas kernels for 0%

profile of v2, /device:TPU:1, one launch (start us, length us, event | category | flops | bytes accessed | tf_op | source)
XLA Modules:
  0.0 182.6 jit_solution(839499954117247904)
XLA Ops:
  0.6 0.0 copy-start
  0.6 0.0 copy-start.3
  0.7 0.5 broadcast.887
  1.2 1.5 reduce.9
  2.7 0.5 fusion.26
  3.2 0.1 convert_bitcast_fusion
  3.3 0.5 slice_reduce_fusion
  3.9 0.1 fusion.94
  4.0 0.7 fusion.24
  4.7 0.1 compare_select_fusion
  4.8 0.2 fusion.29
  5.0 24.0 %scatter_custom_fusion = bf16[16384,128]{1,0:T(8,128)(2,1)} fusion(s32[8192]{0:T(1024)S(1)} %bitcast.109, bf16[8192,128]{1,0:T(8,128)(2,1)} %param.15, bf16[]{:T(256)} %constant.150.clone.1), kind=kCustom, calls=%fused_computation.44 | custom fusion | bytes 4194816 | tf_op jit(solution)/shard_map/scatter | solution.py:73
  29.0 13.3 %all-to-all-start = ((bf16[64,256,128]{2,1,0:T(8,128)(2,1)}), bf16[64,256,128]{2,1,0:T(8,128)(2,1)}, u32[]{:S(2)}, u32[]{:S(2)}) async-start(bf16[64,256,128]{2,1,0:T(8,128)(2,1)} %bitcast.84), calls=%async_computation | async-start | bytes 8388608 | tf_op jit(solution)/shard_map/all_to_all | solution.py:79
  42.3 0.1 fusion.100
  42.4 0.1 fusion.101
  42.6 0.5 select_add_fusion
  43.1 0.2 add_multiply_fusion
  43.3 6.9 %broadcast_multiply_fusion = f32[8192,11,35]{0,2,1:T(8,128)} fusion(f32[8192,35]{0,1:T(8,128)S(1)} %select_add_fusion, f32[8192,11]{0,1:T(8,128)S(1)} %add_multiply_fusion), kind=kLoop, calls=%fused_computation.33 | loop fusion | flops 3153920 | bytes 14123008 | tf_op jit(solution)/shard_map/mul | solution.py:108
  50.2 13.1 %mul.627 = f32[8192,385]{0,1:T(8,128)} reshape(f32[8192,11,35]{0,2,1:T(8,128)} %broadcast_multiply_fusion) | data formatting | bytes 25231360 | tf_op jit(solution)/shard_map/mul | solution.py:108
  63.3 13.2 %dot_general.40 = f32[11,35,8192]{2,1,0:T(8,128)} reshape(f32[385,8192]{1,0:T(8,128)} %bitcast.83) | data formatting | bytes 25231360 | tf_op jit(solution)/shard_map/dot_general | solution.py:110
  76.5 0.1 add_select_fusion.5
  76.6 0.0 copy-start.7
  76.6 0.0 copy-start.8
  76.6 0.0 copy-start.9
  76.7 0.0 copy-start.11
  76.7 29.0 %fusion.1 = f32[11,35,512]{2,1,0:T(8,128)S(1)} fusion(f32[11,35,8192]{2,1,0:T(8,128)} %dot_general.40, f32[8192]{0:T(1024)S(1)} %get-tuple-element.63, s32[8192]{0:T(1024)S(1)} %get-tuple-element.60, f32[8192]{0:T(1024)S(1)} %get-tuple-element.62, s32[8192]{0:T(1024)S(1)} %get-tuple-element.59, f32[8192]{0:T(1024)S(1)} %get-tuple-element.64, ...), kind=kOutput, calls=%fused_computation.3 | convolution fusion | flops 9734979584 | bytes 13666304 | tf_op jit(solution)/shard_map/dot_general | solution.py:110
  105.7 1.6 collective-permute-start
  107.3 0.3 fusion.82
  107.5 0.2 fusion.93
  107.8 0.0 copy-done
  107.8 0.0 copy-done.7
  107.8 4.0 %add_convert_fusion = (bf16[3,8192]{1,0:T(4,128)(2,1)S(1)}, bf16[3,8192]{1,0:T(4,128)(2,1)S(1)}) fusion(f32[3,8192]{1,0:T(4,128)S(1)} %copy-done.7, f32[3,8192]{1,0:T(4,128)S(1)} %copy-done.8, bf16[3,256]{1,0:T(4,128)(2,1)S(1)} %copy-done.11, bf16[8192,128]{1,0:T(8,128)(2,1)} %param.15, bf16[128,256]{1,0:T(8,128)(2,1)S(1)} %copy-done, ...), kind=kOutput, calls=%fused_computation.86 | convolution fusion | flops 560160768 | bytes 2557440 | tf_op jit(solution)/shard_map/dot_general | solution.py:81
  111.9 0.1 pad_maximum_fusion.3
  111.9 0.5 broadcast_multiply_fusion.1
  112.4 2.9 %fusion.34 = bf16[384,256]{1,0:T(8,128)(2,1)} fusion(bf16[384,8192]{1,0:T(8,128)(2,1)S(1)} %bitcast.89, s32[8192]{0:T(1024)S(1)} %bitcast.110), kind=kOutput, calls=%fused_computation.56 | convolution fusion | flops 1612808192 | bytes 6520832 | tf_op jit(solution)/shard_map/dot_general | solution.py:88
  115.3 0.3 multiply_subtract_fusion
  115.7 1.8 %copy.39 = bf16[64,6,256]{0,2,1:T(8,128)(2,1)} copy(bf16[64,6,256]{2,0,1:T(8,128)(2,1)} %bitcast.103) | data formatting | bytes 393216 | tf_op jit(solution)/shard_map/reshape | solution.py:122
  117.5 0.0 collective-permute-done
  117.6 0.3 scatter-add.6
  117.8 1.5 copy.35
  119.3 2.9 %copy.36 = bf16[64,11,32,8]{0,3,2,1:T(8,128)(2,1)} copy(bf16[64,11,32,8]{2,3,0,1:T(8,128)(2,1)} %bitcast.90) | data formatting | bytes 720896 | tf_op jit(solution)/shard_map/transpose | solution.py:124
  122.2 1.5 pad_maximum_fusion.1
  123.7 14.5 %all-to-all-done = bf16[64,256,128]{2,1,0:T(8,128)(2,1)} async-done(((bf16[64,256,128]{2,1,0:T(8,128)(2,1)}), bf16[64,256,128]{2,1,0:T(8,128)(2,1)}, u32[]{:S(2)}, u32[]{:S(2)}) %all-to-all-start) | async-done | bytes 4194336 | tf_op jit(solution)/shard_map/all_to_all | solution.py:79
  138.2 0.5 broadcast.890
  138.7 2.3 %reduce.10 = bf16[64,4352]{0,1:T(8,128)(2,1)} reduce(bf16[64,1,4352]{0,2,1:T(8,128)(2,1)S(1)} %bitcast.91, bf16[]{:T(256)} %broadcast.890), dimensions={1}, to_apply=%copy.38.reduce_sub_computation | reduce | bytes 1114114 | tf_op jit(solution)/shard_map/all_to_all | solution.py:128
  141.0 1.6 copy.46
  142.5 0.9 reshape.823
  143.5 5.9 %all-to-all-start.1 = ((bf16[64,2,2176]{2,1,0:T(2,128)(2,1)}), bf16[64,2,2176]{2,1,0:T(2,128)(2,1)}, u32[]{:S(2)}, u32[]{:S(2)}) async-start(bf16[64,2,2176]{2,1,0:T(2,128)(2,1)} %reshape.823), calls=%async_computation.1 | async-start | bytes 1114112 | tf_op jit(solution)/shard_map/all_to_all | solution.py:128
  149.4 9.5 %fusion = bf16[16384,128]{1,0:T(8,128)(2,1)} fusion(bf16[256,128]{1,0:T(8,128)(2,1)S(1)} %copy-done.10, bf16[16384,128]{1,0:T(8,128)(2,1)} %bitcast.23, bf16[128,256]{1,0:T(8,128)(2,1)S(1)} %copy-done), kind=kOutput, calls=%fused_computation.2 | convolution fusion | flops 2174746624 | bytes 8519680 | tf_op jit(solution)/shard_map/dot_general | solution.py:133
  158.9 8.5 %all-to-all-done.1 = bf16[64,2,2176]{2,1,0:T(2,128)(2,1)} async-done(((bf16[64,2,2176]{2,1,0:T(2,128)(2,1)}), bf16[64,2,2176]{2,1,0:T(2,128)(2,1)}, u32[]{:S(2)}, u32[]{:S(2)}) %all-to-all-start.1) | async-done | bytes 557088 | tf_op jit(solution)/shard_map/all_to_all | solution.py:128
  167.4 3.7 %reshape.824 = bf16[64,1,4352]{2,1,0:T(2,128)(2,1)S(1)} reshape(bf16[64,2,2176]{2,1,0:T(2,128)(2,1)} %all-to-all-done.1) | data formatting | bytes 1114112
  171.1 0.1 copy.45
  171.1 0.8 copy-done.1
  171.9 0.9 slice_convert_fusion
  172.8 1.3 reshape.799
  174.2 1.7 slice_convert_fusion.1
  176.0 0.8 slice_add_fusion
  176.7 2.8 %scatter-add.9 = bf16[64,8,256]{2,1,0:T(8,128)(2,1)S(1)} dynamic-update-slice(bf16[64,8,256]{2,1,0:T(8,128)(2,1)S(1)} %slice.129, bf16[64,3,256]{2,1,0:T(4,128)(2,1)} %slice_add_fusion, s32[]{:T(128)} %constant.154.clone.1, s32[]{:T(128)} %constant.154.clone.1, s32[]{:T(128)} %constant.154.clone.1) | dynamic-update-slice | bytes 196612 | tf_op jit(solution)/shard_map/scatter-add | solution.py:141
  179.5 0.0 copy-start.2
  179.6 0.5 fusion.32
  180.0 0.5 fusion.31
  180.5 0.1 fusion.38
  180.7 0.9 reshape.800
  181.6 1.0 pad_maximum_fusion.2
  (30 shorter events, 0.4 us)
Async XLA Ops:
  0.6 107.1 %copy-start = (bf16[128,256]{1,0:T(8,128)(2,1)S(1)}, bf16[128,256]{1,0:T(8,128)(2,1)}, u32[]{:S(2)}) copy-start(bf16[128,256]{1,0:T(8,128)(2,1)} %param.23) | copy-start | bytes 196612
  0.6 4.1 %copy-start.3 = (s32[8192,1]{0,1:T(1,128)S(1)}, s32[8192,1]{0,1:T(1,128)}, u32[]{:S(2)}) copy-start(s32[8192,1]{0,1:T(1,128)} %param.22) | copy-start | bytes 98308
  29.0 13.3 %copy-start.4 = (s32[3,8192]{1,0:T(4,128)S(1)}, s32[3,8192]{1,0:T(4,128)}, u32[]{:S(2)}) copy-start(s32[3,8192]{1,0:T(4,128)} %param.21) | copy-start | bytes 294916
  29.0 13.4 %copy-start.5 = (f32[3,8192]{1,0:T(4,128)S(1)}, f32[3,8192]{1,0:T(4,128)}, u32[]{:S(2)}) copy-start(f32[3,8192]{1,0:T(4,128)} %param.20) | copy-start | bytes 294916
  29.0 14.1 %copy-start.6 = (f32[8192]{0:T(1024)S(1)}, f32[8192]{0:T(1024)}, u32[]{:S(2)}) copy-start(f32[8192]{0:T(1024)} %param.19) | copy-start | bytes 98308
  29.0 109.2 %all-to-all-start = ((bf16[64,256,128]{2,1,0:T(8,128)(2,1)}), bf16[64,256,128]{2,1,0:T(8,128)(2,1)}, u32[]{:S(2)}, u32[]{:S(2)}) async-start(bf16[64,256,128]{2,1,0:T(8,128)(2,1)} %bitcast.84), calls=%async_computation | async-start | bytes 8388608 | tf_op jit(solution)/shard_map/all_to_all | solution.py:79
  76.6 31.1 %copy-start.7 = (f32[3,8192]{1,0:T(4,128)S(1)}, f32[3,8192]{1,0:T(4,128)}, u32[]{:S(2)}) copy-start(f32[3,8192]{1,0:T(4,128)} %param.16) | copy-start | bytes 294916
  76.6 31.1 %copy-start.8 = (f32[3,8192]{1,0:T(4,128)S(1)}, f32[3,8192]{1,0:T(4,128)}, u32[]{:S(2)}) copy-start(f32[3,8192]{1,0:T(4,128)} %param.18) | copy-start | bytes 294916
  76.6 31.1 %copy-start.9 = (f32[3,8192]{1,0:T(4,128)S(1)}, f32[3,8192]{1,0:T(4,128)}, u32[]{:S(2)}) copy-start(f32[3,8192]{1,0:T(4,128)} %param.17) | copy-start | bytes 294916
  76.7 31.1 %copy-start.11 = (bf16[3,256]{1,0:T(4,128)(2,1)S(1)}, bf16[3,256]{1,0:T(4,128)(2,1)}, u32[]{:S(2)}) copy-start(bf16[3,256]{1,0:T(4,128)(2,1)} %param.25) | copy-start | bytes 4612
  105.7 11.9 %collective-permute-start = (bf16[11,3,512]{2,1,0:T(4,128)(2,1)S(1)}, bf16[11,3,512]{2,1,0:T(4,128)(2,1)S(1)}, u32[]{:S(2)}, u32[]{:S(2)}) collective-permute-start(bf16[11,3,512]{2,1,0:T(4,128)(2,1)S(1)} %slice.151), channel_id=1, source_target_pairs={{0,64},{64,128},{128,192},{192,0},{1,65},{65,129},{129,193},{193,1... | collective-permute-start | bytes 101384 | tf_op jit(solution)/shard_map/ppermute | solution.py:13
  122.2 27.2 %copy-start.10 = (bf16[256,128]{1,0:T(8,128)(2,1)S(1)}, bf16[256,128]{1,0:T(8,128)(2,1)}, u32[]{:S(2)}) copy-start(bf16[256,128]{1,0:T(8,128)(2,1)} %param.24) | copy-start | bytes 196612
  143.5 23.9 %all-to-all-start.1 = ((bf16[64,2,2176]{2,1,0:T(2,128)(2,1)}), bf16[64,2,2176]{2,1,0:T(2,128)(2,1)}, u32[]{:S(2)}, u32[]{:S(2)}) async-start(bf16[64,2,2176]{2,1,0:T(2,128)(2,1)} %reshape.823), calls=%async_computation.1 | async-start | bytes 1114112 | tf_op jit(solution)/shard_map/all_to_all | solution.py:128
  171.1 0.8 copy-start.1
  179.5 1.1 copy-start.2

commit v3 on v2

--- a/solution.py
+++ b/solution.py
@@ -123,9 +123,9 @@
     grid_part = (
         brick.reshape(ext_z, BX, n_col, y_block).transpose(2, 0, 1, 3).reshape(n_col, -1)
     )
-    send = jnp.concatenate([state_part, grid_part], axis=1)
+    send = jnp.concatenate([state_part, grid_part], axis=1).reshape(n_col, 2, -1)
     send, got_feat = lax.optimization_barrier((send, got_feat))
-    got = lax.all_to_all(send, "col", split_axis=0, concat_axis=0, tiled=True)
+    got = lax.all_to_all(send, "col", split_axis=0, concat_axis=0, tiled=True).reshape(n_col, -1)
     arrived = got_feat.reshape(n_col * slots, width)
     arrived_hidden = feature_hidden(arrived, w_in)
     arrived_feat = (
@@ -135,11 +135,10 @@
     arrived_state = (
         got[:, : 6 * slots].reshape(n_col, 6, slots).transpose(1, 0, 2).reshape(6, n_col * slots)
     ).astype(jnp.float32)
-    planes = got[:, 6 * slots :].reshape(n_col, ext_z, BX * y_block).astype(jnp.float32)
-    spill = jnp.roll(planes[:, planes_z:], 1, axis=0)
-    pencil = (
-        planes[:, :planes_z].at[:, :3].add(spill).astype(jnp.bfloat16).reshape(GZ, BX * y_block)
-    )
+    planes = got[:, 6 * slots :].reshape(n_col, ext_z, BX * y_block)
+    spill = jnp.roll(planes[:, planes_z:], 1, axis=0).astype(jnp.float32)
+    top = (planes[:, :3].astype(jnp.float32) + spill).astype(jnp.bfloat16)
+    pencil = jnp.concatenate([top, planes[:, 3:planes_z]], axis=1).reshape(GZ, BX * y_block)
     table = dft_table()
     table_hi = table.astype(jnp.bfloat16)
     table_lo = (table - table_hi.astype(jnp.float32)).astype(jnp.bfloat16)

time: 184 us -> 171 us (0.929)
  local copies, waits for them, and re-layouts: 70.8 us -> 63.4 us
  other arithmetic: 19.9 us -> 15.1 us
    unnamed x31 -> x26, local copies, waits for them, and re-layouts: 7.68 us -> 0.99 us
    scatter-add x1 -> x0, local copies, waits for them, and re-layouts: 2.84 us -> none  [body(): planes[:, :planes_z].at[:, :3].add(spill).astype(jnp.bfloat16)]
    all_to_all x1 -> x0, other arithmetic: 2.29 us -> none  [body(): got = lax.all_to_all(send, 'col', split_axis=0, concat_axis=0, tiled=True)]
    optimization_barrier x0 -> x1, local copies, waits for them, and re-layouts: none -> 1.89 us  [body(): send, got_feat = lax.optimization_barrier((send, got_feat))]
  transfers between devices with their start and end apart: 3 -> 3, of which waited for: 2 -> 2; matrix products, arithmetic and copies ran while one was open for 49% -> 52% of each run, Pallas kernels for 0% -> 0%
where the time goes in v3:
time: 171 us; the launch traced here: 170 us
  local copies, waits for them, and re-layouts  63.4 us (37%)
  matrix products  47.2 us (28%)
  waiting for transfers between devices  22.9 us (13%)
  starting transfers between devices  20.7 us (12%)
  other arithmetic  15.1 us (9%)
    dot_general x1, matrix products, body(): lax.dot_general(kron, rows_y, (((0,), (0,)), ((), ())), precision=lax.Pre...  29.1 us
    scatter x1, local copies, waits for them, and re-layouts, body(): feat_buf = jnp.zeros((n_col * slots, width), jnp.bfloat16).at[slot].set(f...  24 us
    all_to_all x1, waiting for transfers between devices, body(): lax.all_to_all(feat_buf, 'col', split_axis=0, concat_axis=0, tiled=True)  14.4 us
    all_to_all x1, starting transfers between devices, body(): lax.all_to_all(feat_buf, 'col', split_axis=0, concat_axis=0, tiled=True)  13.3 us
    dot_general x1, local copies, waits for them, and re-layouts, body(): lax.dot_general(kron, rows_y, (((0,), (0,)), ((), ())), precision=lax.Pre...  13.2 us
    mul x1, local copies, waits for them, and re-layouts, body(): charge[start:stop][:, None, None] * rows_z[:, :, None] * rows_x[:, None, :]  13.1 us
    dot_general x1, matrix products, body(): jnp.dot(arrived_hidden, w_out, preferred_element_type=jnp.float32)  9.49 us
    all_to_all x1, waiting for transfers between devices, body(): lax.all_to_all(send, 'col', split_axis=0, concat_axis=0, tiled=True)  8.53 us
  transfers between devices with their start and end apart: 3, of which 2 were waited for; matrix products, arithmetic and copies ran while one was open for 52% of the time, Pallas kernels for 0%

profile of v3, /device:TPU:1, one launch (start us, length us, event | category | flops | bytes accessed | tf_op | source)
XLA Modules:
  0.0 170.3 jit_solution(3679900167427148244)
XLA Ops:
  0.6 0.0 copy-start
  0.6 0.0 copy-start.2
  0.7 0.5 broadcast.876
  1.2 1.5 reduce.7
  2.7 0.5 fusion.26
  3.2 0.1 convert_bitcast_fusion
  3.3 0.5 slice_reduce_fusion
  3.9 0.1 fusion.90
  4.0 0.7 fusion.24
  4.7 0.0 copy-done.2
  4.7 0.1 compare_select_fusion
  4.8 0.2 fusion.29
  5.0 24.0 %scatter_custom_fusion = bf16[16384,128]{1,0:T(8,128)(2,1)} fusion(s32[8192]{0:T(1024)S(1)} %bitcast.108, bf16[8192,128]{1,0:T(8,128)(2,1)} %param.13, bf16[]{:T(256)} %constant.127.clone.1), kind=kCustom, calls=%fused_computation.44 | custom fusion | bytes 4194816 | tf_op jit(solution)/shard_map/scatter | solution.py:73
  29.0 13.3 %all-to-all-start = ((bf16[64,256,128]{2,1,0:T(8,128)(2,1)}), bf16[64,256,128]{2,1,0:T(8,128)(2,1)}, u32[]{:S(2)}, u32[]{:S(2)}) async-start(bf16[64,256,128]{2,1,0:T(8,128)(2,1)} %bitcast.82), calls=%async_computation | async-start | bytes 8388608 | tf_op jit(solution)/shard_map/all_to_all | solution.py:79
  42.3 0.0 copy-done.3
  42.3 0.1 fusion.98
  42.4 0.0 copy-done.4
  42.4 0.1 fusion.99
  42.6 0.5 select_add_fusion
  43.1 0.0 copy-done.5
  43.1 0.2 add_multiply_fusion
  43.3 6.9 %broadcast_multiply_fusion = f32[8192,11,35]{0,2,1:T(8,128)} fusion(f32[8192,35]{0,1:T(8,128)S(1)} %select_add_fusion, f32[8192,11]{0,1:T(8,128)S(1)} %add_multiply_fusion), kind=kLoop, calls=%fused_computation.33 | loop fusion | flops 3153920 | bytes 14123008 | tf_op jit(solution)/shard_map/mul | solution.py:108
  50.2 13.1 %mul.627 = f32[8192,385]{0,1:T(8,128)} reshape(f32[8192,11,35]{0,2,1:T(8,128)} %broadcast_multiply_fusion) | data formatting | bytes 25231360 | tf_op jit(solution)/shard_map/mul | solution.py:108
  63.3 13.2 %dot_general.40 = f32[11,35,8192]{2,1,0:T(8,128)} reshape(f32[385,8192]{1,0:T(8,128)} %bitcast.81) | data formatting | bytes 25231360 | tf_op jit(solution)/shard_map/dot_general | solution.py:110
  76.5 0.1 add_select_fusion.5
  76.6 0.0 copy-start.6
  76.6 0.0 copy-start.7
  76.6 0.0 copy-start.8
  76.6 0.0 copy-start.10
  76.7 29.1 %fusion.1 = f32[11,35,512]{2,1,0:T(8,128)S(1)} fusion(f32[11,35,8192]{2,1,0:T(8,128)} %dot_general.40, f32[8192]{0:T(1024)S(1)} %get-tuple-element.51, s32[8192]{0:T(1024)S(1)} %get-tuple-element.48, f32[8192]{0:T(1024)S(1)} %get-tuple-element.50, s32[8192]{0:T(1024)S(1)} %get-tuple-element.47, f32[8192]{0:T(1024)S(1)} %get-tuple-element.52, ...), kind=kOutput, calls=%fused_computation.3 | convolution fusion | flops 9734979584 | bytes 13666304 | tf_op jit(solution)/shard_map/dot_general | solution.py:110
  105.8 1.6 collective-permute-start
  107.4 0.3 fusion.78
  107.7 0.2 fusion.89
  107.9 0.0 copy-done
  107.9 4.0 %add_convert_fusion.1 = (bf16[3,8192]{1,0:T(4,128)(2,1)S(1)}, bf16[3,8192]{1,0:T(4,128)(2,1)S(1)}) fusion(f32[3,8192]{1,0:T(4,128)S(1)} %copy-done.6, f32[3,8192]{1,0:T(4,128)S(1)} %copy-done.7, bf16[3,256]{1,0:T(4,128)(2,1)S(1)} %copy-done.10, bf16[8192,128]{1,0:T(8,128)(2,1)} %param.13, bf16[128,256]{1,0:T(8,128)(2,1)S(1)} %copy-done, ...), kind=kOutput, calls=%fused_computation.81 | convolution fusion | flops 560160768 | bytes 2557440 | tf_op jit(solution)/shard_map/dot_general | solution.py:81
  112.0 0.1 pad_maximum_fusion.3
  112.1 0.5 broadcast_multiply_fusion.1
  112.5 2.9 %fusion.34 = bf16[384,256]{1,0:T(8,128)(2,1)} fusion(bf16[384,8192]{1,0:T(8,128)(2,1)S(1)} %bitcast.87, s32[8192]{0:T(1024)S(1)} %bitcast.109), kind=kOutput, calls=%fused_computation.56 | convolution fusion | flops 1612808192 | bytes 6520832 | tf_op jit(solution)/shard_map/dot_general | solution.py:88
  115.4 0.3 multiply_subtract_fusion
  115.8 1.8 %copy.32 = bf16[64,6,256]{0,2,1:T(8,128)(2,1)} copy(bf16[64,6,256]{2,0,1:T(8,128)(2,1)} %bitcast.102) | data formatting | bytes 393216 | tf_op jit(solution)/shard_map/reshape | solution.py:122
  117.6 0.0 collective-permute-done
  117.7 0.3 scatter-add.4
  117.9 0.0 copy-start.9
  118.0 1.5 copy.28
  119.4 2.9 %copy.29 = bf16[64,11,32,8]{0,3,2,1:T(8,128)(2,1)} copy(bf16[64,11,32,8]{2,3,0,1:T(8,128)(2,1)} %bitcast.88) | data formatting | bytes 720896 | tf_op jit(solution)/shard_map/transpose | solution.py:124
  122.3 1.4 pad_maximum_fusion.1
  123.8 14.4 %all-to-all-done = bf16[64,256,128]{2,1,0:T(8,128)(2,1)} async-done(((bf16[64,256,128]{2,1,0:T(8,128)(2,1)}), bf16[64,256,128]{2,1,0:T(8,128)(2,1)}, u32[]{:S(2)}, u32[]{:S(2)}) %all-to-all-start) | async-done | bytes 4194336 | tf_op jit(solution)/shard_map/all_to_all | solution.py:79
  138.2 1.9 %copy.31 = bf16[64,2,2176]{2,1,0:T(2,128)(2,1)} copy(bf16[64,2,2176]{0,2,1:T(8,128)(2,1)S(1)} %bitcast.89) | data formatting | bytes 1114112 | tf_op jit(solution)/shard_map/optimization_barrier | solution.py:127
  140.1 5.8 %all-to-all-start.1 = ((bf16[64,2,2176]{2,1,0:T(2,128)(2,1)}), bf16[64,2,2176]{2,1,0:T(2,128)(2,1)S(1)}, u32[]{:S(2)}, u32[]{:S(2)}) async-start(bf16[64,2,2176]{2,1,0:T(2,128)(2,1)} %copy.31), calls=%async_computation.1 | async-start | bytes 1114112 | tf_op jit(solution)/shard_map/all_to_all | solution.py:128
  145.8 9.5 %fusion = bf16[16384,128]{1,0:T(8,128)(2,1)} fusion(bf16[256,128]{1,0:T(8,128)(2,1)S(1)} %copy-done.9, bf16[16384,128]{1,0:T(8,128)(2,1)} %bitcast.24, bf16[128,256]{1,0:T(8,128)(2,1)S(1)} %copy-done), kind=kOutput, calls=%fused_computation.2 | convolution fusion | flops 2174746624 | bytes 8519680 | tf_op jit(solution)/shard_map/dot_general | solution.py:133
  155.3 8.5 %all-to-all-done.1 = bf16[64,2,2176]{2,1,0:T(2,128)(2,1)S(1)} async-done(((bf16[64,2,2176]{2,1,0:T(2,128)(2,1)}), bf16[64,2,2176]{2,1,0:T(2,128)(2,1)S(1)}, u32[]{:S(2)}, u32[]{:S(2)}) %all-to-all-start.1) | async-done | bytes 557088 | tf_op jit(solution)/shard_map/all_to_all | solution.py:128
  163.8 0.1 copy.36
  163.9 0.8 slice.106
  164.7 1.2 reshape.774
  165.9 0.1 slice.110
  166.0 0.8 slice_convert_fusion
  166.8 0.1 add_convert_fusion
  166.9 0.5 fusion.32
  167.4 0.0 copy-start.1
  167.4 0.6 fusion.31
  168.0 0.1 fusion.38
  168.1 0.3 copy-done.1
  168.4 0.9 reshape.778
  169.3 1.0 pad_maximum_fusion.2
  (23 shorter events, 0.3 us)
Async XLA Ops:
  0.6 107.3 %copy-start = (bf16[128,256]{1,0:T(8,128)(2,1)S(1)}, bf16[128,256]{1,0:T(8,128)(2,1)}, u32[]{:S(2)}) copy-start(bf16[128,256]{1,0:T(8,128)(2,1)} %param.21) | copy-start | bytes 196612
  0.6 4.1 %copy-start.2 = (s32[8192,1]{0,1:T(1,128)S(1)}, s32[8192,1]{0,1:T(1,128)}, u32[]{:S(2)}) copy-start(s32[8192,1]{0,1:T(1,128)} %param.20) | copy-start | bytes 98308
  29.0 13.3 %copy-start.3 = (s32[3,8192]{1,0:T(4,128)S(1)}, s32[3,8192]{1,0:T(4,128)}, u32[]{:S(2)}) copy-start(s32[3,8192]{1,0:T(4,128)} %param.19) | copy-start | bytes 294916
  29.0 13.4 %copy-start.4 = (f32[3,8192]{1,0:T(4,128)S(1)}, f32[3,8192]{1,0:T(4,128)}, u32[]{:S(2)}) copy-start(f32[3,8192]{1,0:T(4,128)} %param.18) | copy-start | bytes 294916
  29.0 14.1 %copy-start.5 = (f32[8192]{0:T(1024)S(1)}, f32[8192]{0:T(1024)}, u32[]{:S(2)}) copy-start(f32[8192]{0:T(1024)} %param.17) | copy-start | bytes 98308
  29.0 109.2 %all-to-all-start = ((bf16[64,256,128]{2,1,0:T(8,128)(2,1)}), bf16[64,256,128]{2,1,0:T(8,128)(2,1)}, u32[]{:S(2)}, u32[]{:S(2)}) async-start(bf16[64,256,128]{2,1,0:T(8,128)(2,1)} %bitcast.82), calls=%async_computation | async-start | bytes 8388608 | tf_op jit(solution)/shard_map/all_to_all | solution.py:79
  76.6 31.3 %copy-start.6 = (f32[3,8192]{1,0:T(4,128)S(1)}, f32[3,8192]{1,0:T(4,128)}, u32[]{:S(2)}) copy-start(f32[3,8192]{1,0:T(4,128)} %param.14) | copy-start | bytes 294916
  76.6 31.3 %copy-start.7 = (f32[3,8192]{1,0:T(4,128)S(1)}, f32[3,8192]{1,0:T(4,128)}, u32[]{:S(2)}) copy-start(f32[3,8192]{1,0:T(4,128)} %param.16) | copy-start | bytes 294916
  76.6 31.3 %copy-start.8 = (f32[3,8192]{1,0:T(4,128)S(1)}, f32[3,8192]{1,0:T(4,128)}, u32[]{:S(2)}) copy-start(f32[3,8192]{1,0:T(4,128)} %param.15) | copy-start | bytes 294916
  76.6 31.3 %copy-start.10 = (bf16[3,256]{1,0:T(4,128)(2,1)S(1)}, bf16[3,256]{1,0:T(4,128)(2,1)}, u32[]{:S(2)}) copy-start(bf16[3,256]{1,0:T(4,128)(2,1)} %param.23) | copy-start | bytes 4612
  105.8 11.9 %collective-permute-start = (bf16[11,3,512]{2,1,0:T(4,128)(2,1)S(1)}, bf16[11,3,512]{2,1,0:T(4,128)(2,1)S(1)}, u32[]{:S(2)}, u32[]{:S(2)}) collective-permute-start(bf16[11,3,512]{2,1,0:T(4,128)(2,1)S(1)} %slice.128), channel_id=1, source_target_pairs={{0,64},{64,128},{128,192},{192,0},{1,65},{65,129},{129,193},{193,1... | collective-permute-start | bytes 101384 | tf_op jit(solution)/shard_map/ppermute | solution.py:13
  117.9 27.9 %copy-start.9 = (bf16[256,128]{1,0:T(8,128)(2,1)S(1)}, bf16[256,128]{1,0:T(8,128)(2,1)}, u32[]{:S(2)}) copy-start(bf16[256,128]{1,0:T(8,128)(2,1)} %param.22) | copy-start | bytes 196612
  140.1 23.8 %all-to-all-start.1 = ((bf16[64,2,2176]{2,1,0:T(2,128)(2,1)}), bf16[64,2,2176]{2,1,0:T(2,128)(2,1)S(1)}, u32[]{:S(2)}, u32[]{:S(2)}) async-start(bf16[64,2,2176]{2,1,0:T(2,128)(2,1)} %copy.31), calls=%async_computation.1 | async-start | bytes 1114112 | tf_op jit(solution)/shard_map/all_to_all | solution.py:128
  167.4 1.0 copy-start.1

commit v4 on v3

--- a/solution.py
+++ b/solution.py
@@ -139,18 +139,17 @@
     spill = jnp.roll(planes[:, planes_z:], 1, axis=0).astype(jnp.float32)
     top = (planes[:, :3].astype(jnp.float32) + spill).astype(jnp.bfloat16)
     pencil = jnp.concatenate([top, planes[:, 3:planes_z]], axis=1).reshape(GZ, BX * y_block)
-    table = dft_table()
+    norm_scale = 1.0 / jnp.sqrt(jnp.float32(GZ))
+    signs = jnp.array([norm_scale, -norm_scale], jnp.float32)[:, None, None]
+    table = dft_table().reshape(GZ, 2, GZ).transpose(1, 0, 2) * signs
     table_hi = table.astype(jnp.bfloat16)
     table_lo = (table - table_hi.astype(jnp.float32)).astype(jnp.bfloat16)
-    dims = (((0,), (0,)), ((), ()))
-    both = lax.dot_general(
-        pencil, table_hi, dims, preferred_element_type=jnp.float32
-    ) + lax.dot_general(pencil, table_lo, dims, preferred_element_type=jnp.float32)
-    norm_scale = 1.0 / jnp.sqrt(jnp.float32(GZ))
-    both = both.reshape(BX, y_block, 2 * GZ)
-    real_part = both[..., :GZ] * norm_scale
-    imag_part = -both[..., GZ:] * norm_scale
-    spectrum = jnp.stack([real_part, imag_part])
+    pair = jnp.broadcast_to(pencil[None], (2,) + pencil.shape)
+    dims = (((1,), (1,)), ((0,), (0,)))
+    spectrum = lax.dot_general(
+        pair, table_hi, dims, preferred_element_type=jnp.float32
+    ) + lax.dot_general(pair, table_lo, dims, preferred_element_type=jnp.float32)
+    spectrum = spectrum.reshape(2, BX, y_block, GZ)
     return (arrived_feat, arrived_state, spectrum)
 
 

time: 171 us -> 171 us (level)
  no operation moved by 1% of the time
where the time goes in v4:
time: 171 us; the launch traced here: 170 us
  local copies, waits for them, and re-layouts  63.2 us (37%)
  matrix products  48.2 us (28%)
  waiting for transfers between devices  22.9 us (13%)
  starting transfers between devices  20.7 us (12%)
  other arithmetic  14.1 us (8%)
    dot_general x1, matrix products, body(): lax.dot_general(kron, rows_y, (((0,), (0,)), ((), ())), precision=lax.Pre...  29.1 us
    scatter x1, local copies, waits for them, and re-layouts, body(): feat_buf = jnp.zeros((n_col * slots, width), jnp.bfloat16).at[slot].set(f...  24 us
    all_to_all x1, waiting for transfers between devices, body(): lax.all_to_all(feat_buf, 'col', split_axis=0, concat_axis=0, tiled=True)  14.4 us
    all_to_all x1, starting transfers between devices, body(): lax.all_to_all(feat_buf, 'col', split_axis=0, concat_axis=0, tiled=True)  13.3 us
    dot_general x1, local copies, waits for them, and re-layouts, body(): lax.dot_general(kron, rows_y, (((0,), (0,)), ((), ())), precision=lax.Pre...  13.2 us
    mul x1, local copies, waits for them, and re-layouts, body(): charge[start:stop][:, None, None] * rows_z[:, :, None] * rows_x[:, None, :]  13.1 us
    dot_general x1, matrix products, body(): jnp.dot(arrived_hidden, w_out, preferred_element_type=jnp.float32)  9.49 us
    all_to_all x1, waiting for transfers between devices, body(): lax.all_to_all(send, 'col', split_axis=0, concat_axis=0, tiled=True)  8.52 us
  transfers between devices with their start and end apart: 3, of which 2 were waited for; matrix products, arithmetic and copies ran while one was open for 52% of the time, Pallas kernels for 0%

profile of v4, /device:TPU:1, one launch (start us, length us, event | category | flops | bytes accessed | tf_op | source)
XLA Modules:
  0.0 170.2 jit_solution(6012271321187086791)
XLA Ops:
  0.6 0.0 copy-start
  0.6 0.0 copy-start.2
  0.7 0.5 broadcast.871
  1.2 1.5 reduce.7
  2.7 0.5 fusion.27
  3.2 0.1 convert_bitcast_fusion
  3.3 0.5 slice_reduce_fusion
  3.9 0.1 fusion.92
  4.0 0.7 fusion.25
  4.7 0.0 copy-done.2
  4.7 0.1 compare_select_fusion
  4.8 0.2 fusion.30
  5.0 24.0 %scatter_custom_fusion = bf16[16384,128]{1,0:T(8,128)(2,1)} fusion(s32[8192]{0:T(1024)S(1)} %bitcast.112, bf16[8192,128]{1,0:T(8,128)(2,1)} %param.13, bf16[]{:T(256)} %constant.128.clone.1), kind=kCustom, calls=%fused_computation.45 | custom fusion | bytes 4194816 | tf_op jit(solution)/shard_map/scatter | solution.py:73
  29.0 13.3 %all-to-all-start = ((bf16[64,256,128]{2,1,0:T(8,128)(2,1)}), bf16[64,256,128]{2,1,0:T(8,128)(2,1)}, u32[]{:S(2)}, u32[]{:S(2)}) async-start(bf16[64,256,128]{2,1,0:T(8,128)(2,1)} %bitcast.86), calls=%async_computation | async-start | bytes 8388608 | tf_op jit(solution)/shard_map/all_to_all | solution.py:79
  42.3 0.0 copy-done.3
  42.3 0.1 fusion.98
  42.4 0.0 copy-done.4
  42.4 0.1 fusion.99
  42.6 0.5 select_add_fusion
  43.1 0.2 add_multiply_fusion
  43.3 6.9 %broadcast_multiply_fusion = f32[8192,11,35]{0,2,1:T(8,128)} fusion(f32[8192,35]{0,1:T(8,128)S(1)} %select_add_fusion, f32[8192,11]{0,1:T(8,128)S(1)} %add_multiply_fusion), kind=kLoop, calls=%fused_computation.33 | loop fusion | flops 3153920 | bytes 14123008 | tf_op jit(solution)/shard_map/mul | solution.py:108
  50.2 13.1 %mul.660 = f32[8192,385]{0,1:T(8,128)} reshape(f32[8192,11,35]{0,2,1:T(8,128)} %broadcast_multiply_fusion) | data formatting | bytes 25231360 | tf_op jit(solution)/shard_map/mul | solution.py:108
  63.3 13.2 %dot_general.40 = f32[11,35,8192]{2,1,0:T(8,128)} reshape(f32[385,8192]{1,0:T(8,128)} %bitcast.85) | data formatting | bytes 25231360 | tf_op jit(solution)/shard_map/dot_general | solution.py:110
  76.5 0.1 add_select_fusion.5
  76.6 0.0 copy-start.7
  76.6 0.0 copy-start.8
  76.6 0.0 copy-start.9
  76.6 0.0 copy-start.11
  76.7 29.1 %fusion.1 = f32[11,35,512]{2,1,0:T(8,128)S(1)} fusion(f32[11,35,8192]{2,1,0:T(8,128)} %dot_general.40, f32[8192]{0:T(1024)S(1)} %get-tuple-element.49, s32[8192]{0:T(1024)S(1)} %get-tuple-element.46, f32[8192]{0:T(1024)S(1)} %get-tuple-element.48, s32[8192]{0:T(1024)S(1)} %get-tuple-element.45, f32[8192]{0:T(1024)S(1)} %get-tuple-element.50, ...), kind=kOutput, calls=%fused_computation.3 | convolution fusion | flops 9734979584 | bytes 13666304 | tf_op jit(solution)/shard_map/dot_general | solution.py:110
  105.8 1.6 collective-permute-start
  107.4 0.3 fusion.80
  107.7 0.2 fusion.91
  107.9 4.0 %add_convert_fusion.1 = (bf16[3,8192]{1,0:T(4,128)(2,1)S(1)}, bf16[3,8192]{1,0:T(4,128)(2,1)S(1)}) fusion(f32[3,8192]{1,0:T(4,128)S(1)} %copy-done.7, f32[3,8192]{1,0:T(4,128)S(1)} %copy-done.8, bf16[3,256]{1,0:T(4,128)(2,1)S(1)} %copy-done.11, bf16[8192,128]{1,0:T(8,128)(2,1)} %param.13, bf16[128,256]{1,0:T(8,128)(2,1)S(1)} %copy-done, ...), kind=kOutput, calls=%fused_computation.80 | convolution fusion | flops 560160768 | bytes 2557440 | tf_op jit(solution)/shard_map/dot_general | solution.py:81
  112.0 0.1 pad_maximum_fusion.1
  112.1 0.5 broadcast_multiply_fusion.1
  112.5 2.9 %fusion.33 = bf16[384,256]{1,0:T(8,128)(2,1)} fusion(bf16[384,8192]{1,0:T(8,128)(2,1)S(1)} %bitcast.91, s32[8192]{0:T(1024)S(1)} %bitcast.113), kind=kOutput, calls=%fused_computation.56 | convolution fusion | flops 1612808192 | bytes 6520832 | tf_op jit(solution)/shard_map/dot_general | solution.py:88
  115.4 0.3 multiply_subtract_fusion
  115.8 1.8 %copy.43 = bf16[64,6,256]{0,2,1:T(8,128)(2,1)} copy(bf16[64,6,256]{2,0,1:T(8,128)(2,1)} %bitcast.106) | data formatting | bytes 393216 | tf_op jit(solution)/shard_map/reshape | solution.py:122
  117.6 0.0 collective-permute-done
  117.7 0.3 scatter-add.4
  117.9 0.0 copy-start.10
  118.0 1.5 copy.34
  119.4 2.9 %copy.35 = bf16[64,11,32,8]{0,3,2,1:T(8,128)(2,1)} copy(bf16[64,11,32,8]{2,3,0,1:T(8,128)(2,1)} %bitcast.92) | data formatting | bytes 720896 | tf_op jit(solution)/shard_map/transpose | solution.py:124
  122.3 1.4 pad_maximum_fusion
  123.8 14.4 %all-to-all-done = bf16[64,256,128]{2,1,0:T(8,128)(2,1)} async-done(((bf16[64,256,128]{2,1,0:T(8,128)(2,1)}), bf16[64,256,128]{2,1,0:T(8,128)(2,1)}, u32[]{:S(2)}, u32[]{:S(2)}) %all-to-all-start) | async-done | bytes 4194336 | tf_op jit(solution)/shard_map/all_to_all | solution.py:79
  138.2 1.9 %copy.37 = bf16[64,2,2176]{2,1,0:T(2,128)(2,1)} copy(bf16[64,2,2176]{0,2,1:T(8,128)(2,1)S(1)} %bitcast.93) | data formatting | bytes 1114112 | tf_op jit(solution)/shard_map/optimization_barrier | solution.py:127
  140.1 5.8 %all-to-all-start.1 = ((bf16[64,2,2176]{2,1,0:T(2,128)(2,1)}), bf16[64,2,2176]{2,1,0:T(2,128)(2,1)S(1)}, u32[]{:S(2)}, u32[]{:S(2)}) async-start(bf16[64,2,2176]{2,1,0:T(2,128)(2,1)} %copy.37), calls=%async_computation.1 | async-start | bytes 1114112 | tf_op jit(solution)/shard_map/all_to_all | solution.py:128
  145.8 0.0 copy-done.10
  145.8 9.5 %fusion = bf16[16384,128]{1,0:T(8,128)(2,1)} fusion(bf16[256,128]{1,0:T(8,128)(2,1)S(1)} %copy-done.10, bf16[16384,128]{1,0:T(8,128)(2,1)} %bitcast.24, bf16[128,256]{1,0:T(8,128)(2,1)S(1)} %copy-done), kind=kOutput, calls=%fused_computation.2 | convolution fusion | flops 2174746624 | bytes 8519680 | tf_op jit(solution)/shard_map/dot_general | solution.py:133
  155.3 8.5 %all-to-all-done.1 = bf16[64,2,2176]{2,1,0:T(2,128)(2,1)S(1)} async-done(((bf16[64,2,2176]{2,1,0:T(2,128)(2,1)}), bf16[64,2,2176]{2,1,0:T(2,128)(2,1)S(1)}, u32[]{:S(2)}, u32[]{:S(2)}) %all-to-all-start.1) | async-done | bytes 557088 | tf_op jit(solution)/shard_map/all_to_all | solution.py:128
  163.8 0.1 copy.47
  163.9 0.8 slice.98
  164.7 1.2 reshape.849
  165.9 0.1 slice.102
  166.0 0.8 slice_convert_fusion
  166.8 0.1 add_convert_fusion
  166.9 0.1 maximum_bitcast_fusion
  167.0 0.0 copy-start.1
  167.0 0.1 copy.38
  167.2 0.0 copy-done.6
  167.2 0.6 fusion.34
  167.8 1.5 fusion.32
  169.3 0.0 copy-done.1
  169.3 0.9 reshape.852
  (25 shorter events, 0.3 us)
Async XLA Ops:
  0.6 107.3 %copy-start = (bf16[128,256]{1,0:T(8,128)(2,1)S(1)}, bf16[128,256]{1,0:T(8,128)(2,1)}, u32[]{:S(2)}) copy-start(bf16[128,256]{1,0:T(8,128)(2,1)} %param.21) | copy-start | bytes 196612
  0.6 4.1 %copy-start.2 = (s32[8192,1]{0,1:T(1,128)S(1)}, s32[8192,1]{0,1:T(1,128)}, u32[]{:S(2)}) copy-start(s32[8192,1]{0,1:T(1,128)} %param.20) | copy-start | bytes 98308
  29.0 13.3 %copy-start.3 = (s32[3,8192]{1,0:T(4,128)S(1)}, s32[3,8192]{1,0:T(4,128)}, u32[]{:S(2)}) copy-start(s32[3,8192]{1,0:T(4,128)} %param.19) | copy-start | bytes 294916
  29.0 13.4 %copy-start.4 = (f32[3,8192]{1,0:T(4,128)S(1)}, f32[3,8192]{1,0:T(4,128)}, u32[]{:S(2)}) copy-start(f32[3,8192]{1,0:T(4,128)} %param.18) | copy-start | bytes 294916
  29.0 14.1 %copy-start.5 = (f32[8192]{0:T(1024)S(1)}, f32[8192]{0:T(1024)}, u32[]{:S(2)}) copy-start(f32[8192]{0:T(1024)} %param.17) | copy-start | bytes 98308
  29.0 109.2 %all-to-all-start = ((bf16[64,256,128]{2,1,0:T(8,128)(2,1)}), bf16[64,256,128]{2,1,0:T(8,128)(2,1)}, u32[]{:S(2)}, u32[]{:S(2)}) async-start(bf16[64,256,128]{2,1,0:T(8,128)(2,1)} %bitcast.86), calls=%async_computation | async-start | bytes 8388608 | tf_op jit(solution)/shard_map/all_to_all | solution.py:79
  76.6 31.3 %copy-start.7 = (f32[3,8192]{1,0:T(4,128)S(1)}, f32[3,8192]{1,0:T(4,128)}, u32[]{:S(2)}) copy-start(f32[3,8192]{1,0:T(4,128)} %param.14) | copy-start | bytes 294916
  76.6 31.3 %copy-start.8 = (f32[3,8192]{1,0:T(4,128)S(1)}, f32[3,8192]{1,0:T(4,128)}, u32[]{:S(2)}) copy-start(f32[3,8192]{1,0:T(4,128)} %param.16) | copy-start | bytes 294916
  76.6 31.3 %copy-start.9 = (f32[3,8192]{1,0:T(4,128)S(1)}, f32[3,8192]{1,0:T(4,128)}, u32[]{:S(2)}) copy-start(f32[3,8192]{1,0:T(4,128)} %param.15) | copy-start | bytes 294916
  76.6 31.3 %copy-start.11 = (bf16[3,256]{1,0:T(4,128)(2,1)S(1)}, bf16[3,256]{1,0:T(4,128)(2,1)}, u32[]{:S(2)}) copy-start(bf16[3,256]{1,0:T(4,128)(2,1)} %param.23) | copy-start | bytes 4612
  105.8 11.9 %collective-permute-start = (bf16[11,3,512]{2,1,0:T(4,128)(2,1)S(1)}, bf16[11,3,512]{2,1,0:T(4,128)(2,1)S(1)}, u32[]{:S(2)}, u32[]{:S(2)}) collective-permute-start(bf16[11,3,512]{2,1,0:T(4,128)(2,1)S(1)} %slice.110), channel_id=1, source_target_pairs={{0,64},{64,128},{128,192},{192,0},{1,65},{65,129},{129,193},{193,1... | collective-permute-start | bytes 101384 | tf_op jit(solution)/shard_map/ppermute | solution.py:13
  117.9 27.9 %copy-start.10 = (bf16[256,128]{1,0:T(8,128)(2,1)S(1)}, bf16[256,128]{1,0:T(8,128)(2,1)}, u32[]{:S(2)}) copy-start(bf16[256,128]{1,0:T(8,128)(2,1)} %param.22) | copy-start | bytes 196612
  140.1 23.8 %all-to-all-start.1 = ((bf16[64,2,2176]{2,1,0:T(2,128)(2,1)}), bf16[64,2,2176]{2,1,0:T(2,128)(2,1)S(1)}, u32[]{:S(2)}, u32[]{:S(2)}) async-start(bf16[64,2,2176]{2,1,0:T(2,128)(2,1)} %copy.37), calls=%async_computation.1 | async-start | bytes 1114112 | tf_op jit(solution)/shard_map/all_to_all | solution.py:128
  155.3 11.9 %copy-start.6 = (f32[2]{0:T(128)S(1)}, f32[2]{0:T(128)}, u32[]{:S(2)}) copy-start(f32[2]{0:T(128)} %constant.153.clone.1) | copy-start | bytes 28
  167.0 2.3 %copy-start.1 = (f32[64,1536]{1,0:T(8,128)S(1)}, f32[64,1536]{1,0:T(8,128)}, u32[]{:S(2)}) copy-start(f32[64,1536]{1,0:T(8,128)} %slice_convert_fusion) | copy-start | bytes 1179652

commit v5 on v3

--- a/solution.py
+++ b/solution.py
@@ -123,9 +123,11 @@
     grid_part = (
         brick.reshape(ext_z, BX, n_col, y_block).transpose(2, 0, 1, 3).reshape(n_col, -1)
     )
-    send = jnp.concatenate([state_part, grid_part], axis=1).reshape(n_col, 2, -1)
+    send = jnp.concatenate(
+        [state_part.reshape(n_col, 6, slots), grid_part.reshape(n_col, ext_z, BX * y_block)], axis=1
+    )
     send, got_feat = lax.optimization_barrier((send, got_feat))
-    got = lax.all_to_all(send, "col", split_axis=0, concat_axis=0, tiled=True).reshape(n_col, -1)
+    got = lax.all_to_all(send, "col", split_axis=0, concat_axis=0, tiled=True)
     arrived = got_feat.reshape(n_col * slots, width)
     arrived_hidden = feature_hidden(arrived, w_in)
     arrived_feat = (
@@ -133,9 +135,9 @@
         + jnp.dot(arrived_hidden, w_out, preferred_element_type=jnp.float32)
     ).astype(jnp.bfloat16)
     arrived_state = (
-        got[:, : 6 * slots].reshape(n_col, 6, slots).transpose(1, 0, 2).reshape(6, n_col * slots)
+        got[:, :6].transpose(1, 0, 2).reshape(6, n_col * slots)
     ).astype(jnp.float32)
-    planes = got[:, 6 * slots :].reshape(n_col, ext_z, BX * y_block)
+    planes = got[:, 6:]
     spill = jnp.roll(planes[:, planes_z:], 1, axis=0).astype(jnp.float32)
     top = (planes[:, :3].astype(jnp.float32) + spill).astype(jnp.bfloat16)
     pencil = jnp.concatenate([top, planes[:, 3:planes_z]], axis=1).reshape(GZ, BX * y_block)

time: 171 us -> 172 us (level)
  waiting for transfers between devices: 22.9 us -> 27.9 us
  local copies, waits for them, and re-layouts: 63.4 us -> 59.8 us
    all_to_all x1, waiting for transfers between devices: 8.53 us -> 13.4 us  [body(): got = lax.all_to_all(send, 'col', split_axis=0, concat_axis=0, tiled=True)]
where the time goes in v5:
time: 172 us
  local copies, waits for them, and re-layouts  59.8 us (35%)
  matrix products  47.2 us (27%)
  waiting for transfers between devices  27.9 us (16%)
  starting transfers between devices  20.5 us (12%)
  other arithmetic  15.2 us (9%)
    dot_general x1, matrix products, body(): lax.dot_general(kron, rows_y, (((0,), (0,)), ((), ())), precision=lax.Pre...  29.1 us
    scatter x1, local copies, waits for them, and re-layouts, body(): feat_buf = jnp.zeros((n_col * slots, width), jnp.bfloat16).at[slot].set(f...  24 us
    all_to_all x1, waiting for transfers between devices, body(): lax.all_to_all(feat_buf, 'col', split_axis=0, concat_axis=0, tiled=True)  14.5 us
    all_to_all x1, waiting for transfers between devices, body(): got = lax.all_to_all(send, 'col', split_axis=0, concat_axis=0, tiled=True)  13.4 us
    all_to_all x1, starting transfers between devices, body(): lax.all_to_all(feat_buf, 'col', split_axis=0, concat_axis=0, tiled=True)  13.3 us
    dot_general x1, local copies, waits for them, and re-layouts, body(): lax.dot_general(kron, rows_y, (((0,), (0,)), ((), ())), precision=lax.Pre...  13.2 us
    mul x1, local copies, waits for them, and re-layouts, body(): charge[start:stop][:, None, None] * rows_z[:, :, None] * rows_x[:, None, :]  13.2 us
    dot_general x1, matrix products, body(): jnp.dot(arrived_hidden, w_out, preferred_element_type=jnp.float32)  9.47 us
  transfers between devices with their start and end apart: 3, of which 2 were waited for; matrix products, arithmetic and copies ran while one was open for 52% of the time, Pallas kernels for 0%

profile of v5, /device:TPU:1, one launch (start us, length us, event | category | flops | bytes accessed | tf_op | source)
XLA Modules:
  0.0 171.7 jit_solution(15899726614489170617)
XLA Ops:
  0.6 0.0 copy-start
  0.6 0.0 copy-start.1
  0.7 0.5 broadcast.876
  1.2 1.5 reduce.7
  2.7 0.5 fusion.26
  3.2 0.1 convert_bitcast_fusion
  3.3 0.5 slice_reduce_fusion
  3.9 0.1 fusion.90
  4.0 0.7 fusion.24
  4.7 0.0 copy-done.1
  4.7 0.1 compare_select_fusion
  4.8 0.2 fusion.29
  5.0 24.0 %scatter_custom_fusion = bf16[16384,128]{1,0:T(8,128)(2,1)} fusion(s32[8192]{0:T(1024)S(1)} %bitcast.98, bf16[8192,128]{1,0:T(8,128)(2,1)} %param.13, bf16[]{:T(256)} %constant.127.clone.1), kind=kCustom, calls=%fused_computation.44 | custom fusion | bytes 4194816 | tf_op jit(solution)/shard_map/scatter | solution.py:73
  29.0 0.0 copy-start.2
  29.0 13.3 %all-to-all-start = ((bf16[64,256,128]{2,1,0:T(8,128)(2,1)}), bf16[64,256,128]{2,1,0:T(8,128)(2,1)}, u32[]{:S(2)}, u32[]{:S(2)}) async-start(bf16[64,256,128]{2,1,0:T(8,128)(2,1)} %bitcast.76), calls=%async_computation | async-start | bytes 8388608 | tf_op jit(solution)/shard_map/all_to_all | solution.py:79
  42.3 0.0 copy-done.2
  42.3 0.1 fusion.98
  42.4 0.0 copy-done.3
  42.4 0.1 fusion.99
  42.6 0.5 select_add_fusion
  43.1 0.0 copy-done.4
  43.1 0.2 add_multiply_fusion
  43.3 6.9 %broadcast_multiply_fusion = f32[8192,11,35]{0,2,1:T(8,128)} fusion(f32[8192,35]{0,1:T(8,128)S(1)} %select_add_fusion, f32[8192,11]{0,1:T(8,128)S(1)} %add_multiply_fusion), kind=kLoop, calls=%fused_computation.33 | loop fusion | flops 3153920 | bytes 14123008 | tf_op jit(solution)/shard_map/mul | solution.py:108
  50.2 13.2 %mul.627 = f32[8192,385]{0,1:T(8,128)} reshape(f32[8192,11,35]{0,2,1:T(8,128)} %broadcast_multiply_fusion) | data formatting | bytes 25231360 | tf_op jit(solution)/shard_map/mul | solution.py:108
  63.3 13.2 %dot_general.40 = f32[11,35,8192]{2,1,0:T(8,128)} reshape(f32[385,8192]{1,0:T(8,128)} %bitcast.75) | data formatting | bytes 25231360 | tf_op jit(solution)/shard_map/dot_general | solution.py:110
  76.5 0.1 add_select_fusion.5
  76.6 0.0 copy-start.5
  76.6 0.0 copy-start.6
  76.7 0.0 copy-start.7
  76.7 0.0 copy-start.9
  76.7 29.1 %fusion.1 = f32[11,35,512]{2,1,0:T(8,128)S(1)} fusion(f32[11,35,8192]{2,1,0:T(8,128)} %dot_general.40, f32[8192]{0:T(1024)S(1)} %get-tuple-element.51, s32[8192]{0:T(1024)S(1)} %get-tuple-element.48, f32[8192]{0:T(1024)S(1)} %get-tuple-element.50, s32[8192]{0:T(1024)S(1)} %get-tuple-element.47, f32[8192]{0:T(1024)S(1)} %get-tuple-element.52, ...), kind=kOutput, calls=%fused_computation.3 | convolution fusion | flops 9734979584 | bytes 13666304 | tf_op jit(solution)/shard_map/dot_general | solution.py:110
  105.8 1.5 collective-permute-start
  107.3 0.3 fusion.78
  107.5 0.2 fusion.89
  107.8 0.0 copy-done
  107.8 0.0 copy-done.5
  107.8 0.0 copy-done.6
  107.8 0.0 copy-done.7
  107.8 0.0 copy-done.9
  107.8 4.0 %add_convert_fusion.1 = (bf16[3,8192]{1,0:T(4,128)(2,1)S(1)}, bf16[3,8192]{1,0:T(4,128)(2,1)S(1)}) fusion(f32[3,8192]{1,0:T(4,128)S(1)} %copy-done.5, f32[3,8192]{1,0:T(4,128)S(1)} %copy-done.6, bf16[3,256]{1,0:T(4,128)(2,1)S(1)} %copy-done.9, bf16[8192,128]{1,0:T(8,128)(2,1)} %param.13, bf16[128,256]{1,0:T(8,128)(2,1)S(1)} %copy-done, ...), kind=kOutput, calls=%fused_computation.81 | convolution fusion | flops 560160768 | bytes 2557440 | tf_op jit(solution)/shard_map/dot_general | solution.py:81
  111.9 0.1 pad_maximum_fusion.3
  111.9 0.5 broadcast_multiply_fusion.1
  112.4 2.9 %fusion.34 = bf16[384,256]{1,0:T(8,128)(2,1)} fusion(bf16[384,8192]{1,0:T(8,128)(2,1)S(1)} %bitcast.81, s32[8192]{0:T(1024)S(1)} %bitcast.99), kind=kOutput, calls=%fused_computation.56 | convolution fusion | flops 1612808192 | bytes 6520832 | tf_op jit(solution)/shard_map/dot_general | solution.py:88
  115.3 0.3 multiply_subtract_fusion
  115.7 1.8 %copy.31 = bf16[6,64,256]{1,2,0:T(8,128)(2,1)} copy(bf16[6,64,256]{2,1,0:T(8,128)(2,1)} %bitcast.92) | data formatting | bytes 393216 | tf_op jit(solution)/shard_map/reshape | solution.py:90
  117.5 0.0 collective-permute-done
  117.6 0.3 scatter-add.4
  117.8 1.5 copy.32
  119.3 2.9 %copy.33 = bf16[64,11,32,8]{0,3,2,1:T(8,128)(2,1)} copy(bf16[64,11,32,8]{2,3,0,1:T(8,128)(2,1)} %bitcast.82) | data formatting | bytes 720896 | tf_op jit(solution)/shard_map/transpose | solution.py:124
  122.3 1.4 pad_maximum_fusion.1
  123.7 14.5 %all-to-all-done = bf16[64,256,128]{2,1,0:T(8,128)(2,1)} async-done(((bf16[64,256,128]{2,1,0:T(8,128)(2,1)}), bf16[64,256,128]{2,1,0:T(8,128)(2,1)}, u32[]{:S(2)}, u32[]{:S(2)}) %all-to-all-start) | async-done | bytes 4194336 | tf_op jit(solution)/shard_map/all_to_all | solution.py:79
  138.2 1.5 copy.34
  139.6 5.8 %all-to-all-start.1 = ((bf16[64,17,256]{2,1,0:T(8,128)(2,1)}), bf16[64,17,256]{2,1,0:T(8,128)(2,1)S(1)}, u32[]{:S(2)}, u32[]{:S(2)}) async-start(bf16[64,17,256]{2,1,0:T(8,128)(2,1)} %copy.34), calls=%async_computation.1 | async-start | bytes 1572864 | tf_op jit(solution)/shard_map/all_to_all | solution.py:130
  145.4 0.0 copy-done.8
  145.4 9.5 %fusion = bf16[16384,128]{1,0:T(8,128)(2,1)} fusion(bf16[256,128]{1,0:T(8,128)(2,1)S(1)} %copy-done.8, bf16[16384,128]{1,0:T(8,128)(2,1)} %bitcast.22, bf16[128,256]{1,0:T(8,128)(2,1)S(1)} %copy-done), kind=kOutput, calls=%fused_computation.2 | convolution fusion | flops 2174746624 | bytes 8519680 | tf_op jit(solution)/shard_map/dot_general | solution.py:135
  154.9 13.4 %all-to-all-done.1 = bf16[64,17,256]{2,1,0:T(8,128)(2,1)S(1)} async-done(((bf16[64,17,256]{2,1,0:T(8,128)(2,1)}), bf16[64,17,256]{2,1,0:T(8,128)(2,1)S(1)}, u32[]{:S(2)}, u32[]{:S(2)}) %all-to-all-start.1) | async-done | bytes 557088 | tf_op jit(solution)/shard_map/all_to_all | solution.py:130
  168.3 0.1 slice.108
  168.4 0.1 slice.109
  168.5 0.1 add_convert_fusion
  168.6 0.5 fusion.32
  169.1 0.6 fusion.31
  169.7 0.1 fusion.38
  169.8 1.0 pad_maximum_fusion.2
  170.9 0.8 slice_convert_fusion
  (17 shorter events, 0.3 us)
Async XLA Ops:
  0.6 107.1 %copy-start = (bf16[128,256]{1,0:T(8,128)(2,1)S(1)}, bf16[128,256]{1,0:T(8,128)(2,1)}, u32[]{:S(2)}) copy-start(bf16[128,256]{1,0:T(8,128)(2,1)} %param.21) | copy-start | bytes 196612
  0.6 4.1 %copy-start.1 = (s32[8192,1]{0,1:T(1,128)S(1)}, s32[8192,1]{0,1:T(1,128)}, u32[]{:S(2)}) copy-start(s32[8192,1]{0,1:T(1,128)} %param.20) | copy-start | bytes 98308
  29.0 13.3 %copy-start.2 = (s32[3,8192]{1,0:T(4,128)S(1)}, s32[3,8192]{1,0:T(4,128)}, u32[]{:S(2)}) copy-start(s32[3,8192]{1,0:T(4,128)} %param.19) | copy-start | bytes 294916
  29.0 13.4 %copy-start.3 = (f32[3,8192]{1,0:T(4,128)S(1)}, f32[3,8192]{1,0:T(4,128)}, u32[]{:S(2)}) copy-start(f32[3,8192]{1,0:T(4,128)} %param.18) | copy-start | bytes 294916
  29.0 14.1 %copy-start.4 = (f32[8192]{0:T(1024)S(1)}, f32[8192]{0:T(1024)}, u32[]{:S(2)}) copy-start(f32[8192]{0:T(1024)} %param.17) | copy-start | bytes 98308
  29.0 109.2 %all-to-all-start = ((bf16[64,256,128]{2,1,0:T(8,128)(2,1)}), bf16[64,256,128]{2,1,0:T(8,128)(2,1)}, u32[]{:S(2)}, u32[]{:S(2)}) async-start(bf16[64,256,128]{2,1,0:T(8,128)(2,1)} %bitcast.76), calls=%async_computation | async-start | bytes 8388608 | tf_op jit(solution)/shard_map/all_to_all | solution.py:79
  76.6 31.1 %copy-start.5 = (f32[3,8192]{1,0:T(4,128)S(1)}, f32[3,8192]{1,0:T(4,128)}, u32[]{:S(2)}) copy-start(f32[3,8192]{1,0:T(4,128)} %param.14) | copy-start | bytes 294916
  76.6 31.1 %copy-start.6 = (f32[3,8192]{1,0:T(4,128)S(1)}, f32[3,8192]{1,0:T(4,128)}, u32[]{:S(2)}) copy-start(f32[3,8192]{1,0:T(4,128)} %param.16) | copy-start | bytes 294916
  76.7 31.1 %copy-start.7 = (f32[3,8192]{1,0:T(4,128)S(1)}, f32[3,8192]{1,0:T(4,128)}, u32[]{:S(2)}) copy-start(f32[3,8192]{1,0:T(4,128)} %param.15) | copy-start | bytes 294916
  76.7 31.1 %copy-start.9 = (bf16[3,256]{1,0:T(4,128)(2,1)S(1)}, bf16[3,256]{1,0:T(4,128)(2,1)}, u32[]{:S(2)}) copy-start(bf16[3,256]{1,0:T(4,128)(2,1)} %param.23) | copy-start | bytes 4612
  105.8 11.7 %collective-permute-start = (bf16[11,3,512]{2,1,0:T(4,128)(2,1)S(1)}, bf16[11,3,512]{2,1,0:T(4,128)(2,1)S(1)}, u32[]{:S(2)}, u32[]{:S(2)}) collective-permute-start(bf16[11,3,512]{2,1,0:T(4,128)(2,1)S(1)} %slice.127), channel_id=1, source_target_pairs={{0,64},{64,128},{128,192},{192,0},{1,65},{65,129},{129,193},{193,1... | collective-permute-start | bytes 101384 | tf_op jit(solution)/shard_map/ppermute | solution.py:13
  119.3 26.1 %copy-start.8 = (bf16[256,128]{1,0:T(8,128)(2,1)S(1)}, bf16[256,128]{1,0:T(8,128)(2,1)}, u32[]{:S(2)}) copy-start(bf16[256,128]{1,0:T(8,128)(2,1)} %param.22) | copy-start | bytes 196612
  139.6 28.7 %all-to-all-start.1 = ((bf16[64,17,256]{2,1,0:T(8,128)(2,1)}), bf16[64,17,256]{2,1,0:T(8,128)(2,1)S(1)}, u32[]{:S(2)}, u32[]{:S(2)}) async-start(bf16[64,17,256]{2,1,0:T(8,128)(2,1)} %copy.34), calls=%async_computation.1 | async-start | bytes 1572864 | tf_op jit(solution)/shard_map/all_to_all | solution.py:130
